TPU v7x, 32 devices: a whole 2x2x4 slice. The times are simulated.
32 devices in a mesh: ctx: 16 (over z, x, core), hg: 2 (over y).
Axes of the slice: x: 2, y: 2, z: 4, core: 2. Of those that a mesh axis runs over, the one named last changes fastest.
Arguments:
- queries: bfloat16 [4096, 2048], P(('ctx', 'hg')), may hold values from -6 to 6
- keys: bfloat16 [4096, 2048], P(('ctx', 'hg')), may hold values from -6 to 6
- values: bfloat16 [4096, 2048], P(('ctx', 'hg')), may hold values from -6 to 6
- reflect_ids: int32 [4096, 16], P('ctx', 'hg'), may hold values from 0 to 1023
- reflect_bank: bfloat16 [1024, 2048], P(None, 'hg'), may hold values from -6 to 6
- out_weight: bfloat16 [2048, 4096], P('hg'), may hold values from -0.125 to 0.125
Outputs:
- mixed: bfloat16 [4096, 4096], P(('ctx', 'hg'))
All inputs are finite; a program needn't handle non-finite values.
Results may differ from a plain program's by a relative error of at most 0.013.
The roundings to bfloat16 on the way count: a program that leaves them out, or rounds other values in their place, can miss the bound.
Values may be sent and summed in bfloat16 or wider, within the bound.
No kernel may reach another device: no remote copies, remote signals or barrier semaphores. Data moves between devices by JAX's collectives and lax.ppermute only.
A program may use at most 192 MiB of HBM per device.

v0:
```python
import math

import jax
import jax.numpy as jnp
from jax import lax
from jax.experimental import pallas as pl
from jax.experimental.pallas import tpu as pltpu
from jax.sharding import PartitionSpec as P

HDIM = 128
BLK = 32
HP = lax.Precision.HIGHEST


def mm(a, b):
    return jnp.einsum("...ij,...jk->...ik", a, b, precision=HP)


def invert_unit_upper(strict):
    eye_blk = jnp.eye(strict.shape[-1], dtype=jnp.float32)
    result = eye_blk - strict
    power = strict
    steps = strict.shape[-1].bit_length()
    for level in range(steps):
        power = mm(power, power)
        result = mm(result, eye_blk + power)
    return result


def exclusive_blocks(mats):
    heads, n, d, _ = mats.shape
    eye = jnp.broadcast_to(jnp.eye(d, dtype=jnp.float32), (heads, 1, d, d))
    acc = jnp.concatenate([eye, mats[:, :-1]], axis=1)
    shift = 1
    while shift < n:
        earlier = jnp.concatenate(
            [jnp.broadcast_to(eye, (heads, shift, d, d)), acc[:, : n - shift]], axis=1
        )
        acc = mm(earlier, acc)
        shift *= 2
    return acc, mm(acc[:, -1], mats[:, -1])


def exclusive_shards(mat, axis):
    length, here = lax.axis_size(axis), lax.axis_index(axis)
    eye = jnp.broadcast_to(jnp.eye(mat.shape[-1], dtype=jnp.float32), mat.shape)
    if length == 1:
        return eye
    acc = lax.ppermute(mat, axis, [(i, i + 1) for i in range(length - 1)])
    acc = jnp.where(here >= 1, acc, eye)
    shift = 1
    while shift < length:
        earlier = lax.ppermute(acc, axis, [(i, i + shift) for i in range(length - shift)])
        acc = jnp.where(here >= shift, mm(earlier, acc), acc)
        shift *= 2
    return acc


def flash_attend(q_glob, k_all, v_all, shard, heads):
    rows, width = q_glob.shape
    nk = k_all.shape[0] // rows
    scale = 1.0 / math.sqrt(HDIM)

    def kernel(c_ref, q_ref, k_ref, v_ref, o_ref, m_sc, l_sc, acc_sc):
        j = pl.program_id(0)
        c = c_ref[0]

        @pl.when(j == 0)
        def _():
            m_sc[...] = jnp.full(m_sc.shape, -1e30, jnp.float32)
            l_sc[...] = jnp.zeros(l_sc.shape, jnp.float32)
            acc_sc[...] = jnp.zeros(acc_sc.shape, jnp.float32)

        def step(masked):
            for hh in range(heads):
                sl = slice(hh * HDIM, (hh + 1) * HDIM)
                qh = q_ref[:, sl]
                kh = k_ref[:, sl]
                vh = v_ref[:, sl]
                s = (
                    lax.dot_general(
                        qh, kh, (((1,), (1,)), ((), ())), preferred_element_type=jnp.float32
                    )
                    * scale
                )
                if masked:
                    row = lax.broadcasted_iota(jnp.int32, s.shape, 0)
                    col = lax.broadcasted_iota(jnp.int32, s.shape, 1)
                    allowed = col <= row
                    s = jnp.where(allowed, s, -1e30)
                m_prev = m_sc[hh]
                m_new = jnp.maximum(m_prev, jnp.max(s, axis=1, keepdims=True))
                p = jnp.exp(s - m_new)
                if masked:
                    p = jnp.where(allowed, p, 0.0)
                fade = jnp.exp(m_prev - m_new)
                l_sc[hh] = l_sc[hh] * fade + jnp.sum(p, axis=1, keepdims=True)
                acc_sc[hh] = acc_sc[hh] * fade + jnp.dot(
                    p.astype(jnp.bfloat16), vh, preferred_element_type=jnp.float32
                )
                m_sc[hh] = m_new

        @pl.when(j < c)
        def _():
            step(False)

        @pl.when(j == c)
        def _():
            step(True)

        @pl.when(j == nk - 1)
        def _():
            for hh in range(heads):
                sl = slice(hh * HDIM, (hh + 1) * HDIM)
                o_ref[:, sl] = (acc_sc[hh] / l_sc[hh]).astype(o_ref.dtype)

    grid_spec = pltpu.PrefetchScalarGridSpec(
        num_scalar_prefetch=1,
        grid=(nk,),
        in_specs=[
            pl.BlockSpec((rows, width), lambda j, c: (0, 0)),
            pl.BlockSpec((rows, width), lambda j, c: (jnp.minimum(j, c[0]), 0)),
            pl.BlockSpec((rows, width), lambda j, c: (jnp.minimum(j, c[0]), 0)),
        ],
        out_specs=pl.BlockSpec((rows, width), lambda j, c: (0, 0)),
        scratch_shapes=[
            pltpu.VMEM((heads, rows, 1), jnp.float32),
            pltpu.VMEM((heads, rows, 1), jnp.float32),
            pltpu.VMEM((heads, rows, HDIM), jnp.float32),
        ],
    )
    return pl.pallas_call(
        kernel,
        grid_spec=grid_spec,
        out_shape=jax.ShapeDtypeStruct((rows, width), jnp.bfloat16),
        compiler_params=pltpu.CompilerParams(dimension_semantics=("arbitrary",)),
    )(jnp.reshape(shard, (1,)).astype(jnp.int32), q_glob, k_all, v_all)


def local(queries, keys, values, reflect_ids, reflect_bank, out_weight):
    groups = lax.axis_size("hg")
    heads = reflect_ids.shape[1]
    width = heads * HDIM
    stacked = jnp.stack([queries, keys, values], axis=1).reshape(
        queries.shape[0], 3, groups, width
    )
    swapped = lax.all_to_all(stacked, "hg", split_axis=2, concat_axis=0, tiled=True)
    rows = swapped.shape[0]
    q_local = swapped[:, 0, 0]
    k_local = swapped[:, 1, 0]
    v_local = swapped[:, 2, 0]
    v_all = lax.all_gather(v_local, "ctx", axis=0, tiled=True)

    nblocks = rows // BLK
    bank = reflect_bank.shape[0]
    table = reflect_bank.reshape(bank, heads, HDIM).transpose(1, 0, 2)
    onehot = (
        reflect_ids.T[:, :, None] == lax.broadcasted_iota(jnp.int32, (1, 1, bank), 2)
    ).astype(reflect_bank.dtype)
    chosen = jnp.einsum(
        "htb,hbd->htd", onehot, table, preferred_element_type=jnp.float32
    )
    vectors = chosen * lax.rsqrt(jnp.sum(chosen * chosen, axis=-1, keepdims=True) + 1e-06)
    blocks = vectors.reshape(heads, nblocks, BLK, HDIM)
    gram = jnp.einsum("hnkd,hnjd->hnkj", blocks, blocks, precision=HP)
    coupling = 2.0 * jnp.triu(gram, 1)
    tri_factor = 2.0 * invert_unit_upper(coupling)
    spread = jnp.einsum("hnkj,hnje->hnke", tri_factor, blocks, precision=HP)
    eye_d = jnp.eye(HDIM, dtype=jnp.float32)
    block_mats = eye_d - jnp.einsum("hnkd,hnke->hnde", blocks, spread, precision=HP)
    lower_mask = jnp.tril(jnp.ones((BLK, BLK), dtype=jnp.bool_))

    inner_prefix, shard_prod = exclusive_blocks(block_mats)
    earlier_prod = exclusive_shards(shard_prod, "ctx")

    def in_shard(matrix):
        split = matrix.astype(jnp.float32).reshape(nblocks, BLK, heads, HDIM).transpose(2, 0, 1, 3)
        proj = jnp.einsum("hnid,hnkd->hnik", split, blocks, precision=HP)
        proj = jnp.where(lower_mask, proj, 0.0)
        coef = jnp.einsum("hnik,hnrk->hnir", proj, tri_factor, precision=HP)
        inblock = split - jnp.einsum("hnir,hnrd->hnid", coef, blocks, precision=HP)
        moved = jnp.einsum("hnid,hned->hnie", inblock, inner_prefix, precision=HP)
        return moved.reshape(heads, rows, HDIM)

    def to_global(moved):
        full = jnp.einsum("hie,hfe->hif", moved, earlier_prod, precision=HP)
        return full.transpose(1, 0, 2).reshape(rows, width).astype(jnp.bfloat16)

    k_glob = to_global(in_shard(k_local))
    k_all = lax.all_gather(k_glob, "ctx", axis=0, tiled=True)
    q_glob = to_global(in_shard(q_local))

    attn = flash_attend(q_glob, k_all, v_all, lax.axis_index("ctx"), heads)
    return lax.psum_scatter(
        jnp.dot(attn, out_weight, preferred_element_type=jnp.float32).astype(jnp.bfloat16),
        "hg",
        scatter_dimension=0,
        tiled=True,
    )


def solution(mesh):
    placed = (
        P(("ctx", "hg"), None),
        P(("ctx", "hg"), None),
        P(("ctx", "hg"), None),
        P("ctx", "hg"),
        P(None, "hg"),
        P("hg", None),
    )
    return jax.shard_map(
        local, mesh=mesh, in_specs=placed, out_specs=P(("ctx", "hg"), None), check_vma=False
    )
```

profile of v0, /device:TPU:27, one launch (start us, length us, event | category | flops | bytes accessed | tf_op | source)
XLA Modules:
  0.0 361.9 jit_solution(16231627286196531540)
XLA Ops:
  6.5 1.5 copy.21
  8.0 1.3 copy.22
  9.3 2.0 copy.23
  11.4 2.4 pad_maximum_fusion.4
  13.8 2.6 copy.24
  16.4 22.3 %all_to_all.18 = bf16[128,3,2,1024]{3,0,1,2:T(8,128)(2,1)S(1)} all-to-all(bf16[128,3,2,1024]{3,0,1,2:T(8,128)(2,1)} %copy.24), channel_id=1, replica_groups=mesh['ctx'=16,'hg'=2] {'hg'}, dimensions={2} | all-to-all | bytes 3145728 | tf_op jit(solution)/shard_map/all_to_all | solution.py:147
  40.1 2.2 multiply_reduce_fusion
  42.6 1.8 fusion.14
  44.4 1.2 fusion.42
  45.6 1.2 fusion.43
  46.7 1.2 fusion.44
  47.9 1.2 fusion.45
  49.1 1.2 fusion.46
  50.3 1.2 fusion.23
  51.5 1.2 fusion.21
  52.7 1.2 fusion.19
  53.9 1.4 fusion.17
  56.5 1.2 fusion.15
  57.6 1.2 convolution_multiply_fusion
  58.8 1.2 fusion.48
  60.0 7.1 %convolution_subtract_fusion = f32[8,8,128,128]{3,2,1,0:T(8,128)S(1)} fusion(f32[8,8,32,128]{3,2,1,0:T(8,128)S(1)} %bitcast.117, f32[8,8,32,128]{3,2,1,0:T(8,128)S(1)} %fusion.48, f32[128,128]{1,0:T(8,128)S(1)} %fusion.36), kind=kOutput, calls=%fused_computation.19 | convolution fusion | flops 403701760 | bytes 6356992 | tf_op jit(solution)/shard_map/hnkd,hnke->hnde/dot_general | solution.py:170
  68.0 4.7 %fusion.1 = f32[8,8,128,128]{3,2,1,0:T(8,128)S(1)} fusion(f32[8,1,128,128]{3,2,1,0:T(8,128)S(1)} %broadcast_in_dim.41, f32[8,7,128,128]{3,2,1,0:T(8,128)S(1)} %slice.37, f32[8,7,128,128]{3,2,1,0:T(8,128)S(1)} %fusion.12), kind=kOutput, calls=%fused_computation.7 | convolution fusion | flops 1612709888 | bytes 12058624 | tf_op jit(solution)/shard_map/...ij,...jk->...ik/dot_general | solution.py:16
  73.1 4.7 %fusion.3 = f32[8,8,128,128]{3,2,1,0:T(8,128)S(1)} fusion(f32[8,8,128,128]{3,2,1,0:T(8,128)S(1)} %fusion.1, f32[8,6,128,128]{3,2,1,0:T(8,128)S(1)} %slice.40, f32[8,2,128,128]{3,2,1,0:T(8,128)S(1)} %broadcast_in_dim_broadcast_in_dim.7), kind=kOutput, calls=%fused_computation.9 | convolution fusion | flops 1611661312 | bytes 12582912 | tf_op jit(solution)/shard_map/...ij,...jk->...ik/dot_general | solution.py:16
  78.3 4.9 %fusion.7 = f32[8,8,128,128]{3,2,1,0:T(8,128)S(1)} fusion(f32[8,8,128,128]{3,2,1,0:T(8,128)S(1)} %fusion.3, f32[8,4,128,128]{3,2,1,0:T(8,128)S(1)} %slice.41, f32[8,4,128,128]{3,2,1,0:T(8,128)S(1)} %broadcast_in_dim_broadcast_in_dim.6), kind=kOutput, calls=%fused_computation.13 | convolution fusion | flops 1611661312 | bytes 12582912 | tf_op jit(solution)/shard_map/...ij,...jk->...ik/dot_general | solution.py:16
  83.2 2.0 copy-done.2
  85.8 1.3 collective-permute-start
  87.1 3.7 %collective-permute-done = f32[8,128,128]{2,1,0:T(8,128)} collective-permute-done((f32[8,128,128]{2,1,0:T(8,128)S(1)}, f32[8,128,128]{2,1,0:T(8,128)}, u32[]{:S(2)}, u32[]{:S(2)}) %collective-permute-start) | collective-permute-done | bytes 524320 | tf_op jit(solution)/shard_map/ppermute | solution.py:49
  91.9 1.3 collective-permute-start.1
  93.2 15.9 %collective-permute-done.1 = f32[8,128,128]{2,1,0:T(8,128)S(1)} collective-permute-done((f32[8,128,128]{2,1,0:T(8,128)S(1)}, f32[8,128,128]{2,1,0:T(8,128)S(1)}, u32[]{:S(2)}, u32[]{:S(2)}) %collective-permute-start.1) | collective-permute-done | bytes 524320 | tf_op jit(solution)/shard_map/ppermute | solution.py:53
  109.7 1.3 collective-permute-start.2
  112.2 12.2 %collective-permute-done.2 = f32[8,128,128]{2,1,0:T(8,128)} collective-permute-done((f32[8,128,128]{2,1,0:T(8,128)S(1)}, f32[8,128,128]{2,1,0:T(8,128)}, u32[]{:S(2)}, u32[]{:S(2)}) %collective-permute-start.2) | collective-permute-done | bytes 524320 | tf_op jit(solution)/shard_map/ppermute | solution.py:53
  124.4 1.7 convolution_select_fusion.5
  126.1 1.3 collective-permute-start.3
  128.3 1.8 fusion.50
  130.1 19.1 %collective-permute-done.3 = f32[8,128,128]{2,1,0:T(8,128)S(1)} collective-permute-done((f32[8,128,128]{2,1,0:T(8,128)S(1)}, f32[8,128,128]{2,1,0:T(8,128)S(1)}, u32[]{:S(2)}, u32[]{:S(2)}) %collective-permute-start.3) | collective-permute-done | bytes 524320 | tf_op jit(solution)/shard_map/ppermute | solution.py:53
  149.9 1.5 collective-permute-start.4
  151.4 1.2 convolution_subtract_fusion.1
  152.7 6.7 %fusion.51 = f32[8,8,32,128]{3,2,1,0:T(8,128)S(1)} fusion(f32[8,8,32,128]{3,2,1,0:T(8,128)S(1)} %convolution_subtract_fusion.1, f32[8,8,128,128]{3,2,1,0:T(8,128)S(1)} %copy-done.3), kind=kOutput, calls=%fused_computation.84 | convolution fusion | flops 402653184 | bytes 6291456 | tf_op jit(solution)/shard_map/hnid,hned->hnie/dot_general | solution.py:182
  159.4 17.4 %collective-permute-done.4 = f32[8,128,128]{2,1,0:T(8,128)S(1)} collective-permute-done((f32[8,128,128]{2,1,0:T(8,128)S(1)}, f32[8,128,128]{2,1,0:T(8,128)S(1)}, u32[]{:S(2)}, u32[]{:S(2)}) %collective-permute-start.4) | collective-permute-done | bytes 524320 | tf_op jit(solution)/shard_map/ppermute | solution.py:53
  177.5 1.9 convolution_convert_fusion.1
  179.4 2.0 copy.32
  182.8 1.8 fusion.47
  184.6 1.2 convolution_subtract_fusion.2
  185.8 6.8 %fusion.49 = f32[8,8,32,128]{3,2,1,0:T(8,128)S(1)} fusion(f32[8,8,32,128]{3,2,1,0:T(8,128)S(1)} %convolution_subtract_fusion.2, f32[8,8,128,128]{3,2,1,0:T(8,128)S(1)} %copy-done.4), kind=kOutput, calls=%fused_computation.82 | convolution fusion | flops 402653184 | bytes 6291456 | tf_op jit(solution)/shard_map/hnid,hned->hnie/dot_general | solution.py:182
  194.7 61.6 %all-gather.4.cloned.1.call-done.k_ref = bf16[4096,1024]{1,0:T(8,128)(2,1)} async-done(((bf16[256,1024]{1,0:T(8,128)(2,1)}), bf16[4096,1024]{1,0:T(8,128)(2,1)}) %all-gather.4.cloned.1.call-update) | async-done | bytes 8388624 | tf_op jit(solution)/shard_map/all_gather | solution.py:190
  256.3 58.9 %shard_map.64 = bf16[256,1024]{1,0:T(8,128)(2,1)} custom-call(s32[1]{0:T(128)} %bitcast.c_ref, bf16[256,1024]{1,0:T(8,128)(2,1)} %copy.31.q_ref, bf16[4096,1024]{1,0:T(8,128)(2,1)} %all-gather.4.cloned.1.call-done.k_ref, bf16[4096,1024]{1,0:T(8,128)(2,1)} %bitcast.122), custom_call_target="tpu_custom_call" | custom-call | tf_op jit(solution)/shard_map/pallas_call | solution.py:132
  315.2 7.4 %convolution_convert_fusion = bf16[256,4096]{1,0:T(8,128)(2,1)} fusion(bf16[256,1024]{1,0:T(8,128)(2,1)} %shard_map.64, bf16[1024,4096]{1,0:T(8,128)(2,1)} %param.11), kind=kOutput, calls=%fused_computation.5 | convolution fusion | flops 2148532224 | bytes 11010048 | tf_op jit(solution)/shard_map/dot_general | solution.py:195
  322.6 32.3 %reduce-scatter.2.cloned.1.call-done = bf16[128,4096]{1,0:T(8,128)(2,1)} async-done(((bf16[256,4096]{1,0:T(8,128)(2,1)}), bf16[128,4096]{1,0:T(8,128)(2,1)}) %reduce-scatter.2.cloned.1.call-update) | async-done | bytes 1048592 | tf_op jit(solution)/shard_map/reduce_scatter | solution.py:194
  (44 shorter events, 13.9 us)
Async XLA Ops:
  6.5 33.5 %copy-start = (bf16[1024,1024]{1,0:T(8,128)(2,1)S(1)}, bf16[1024,1024]{1,0:T(8,128)(2,1)}, u32[]{:S(2)}) copy-start(bf16[1024,1024]{1,0:T(8,128)(2,1)} %param.10) | copy-start | bytes 6291460
  6.5 188.1 %all-gather.6.cloned.1.call-start = ((), (), s32[]{:S(2)}) async-start(), calls=%async_computation.4 | async-start | bytes 8912896 | tf_op jit(solution)/shard_map/all_gather | solution.py:152
  38.6 1.4 copy-start.5
  40.0 216.3 %all-gather.4.cloned.1.call-start = ((), (), s32[]{:S(2)}) async-start(), calls=%async_computation.2 | async-start | bytes 8912896 | tf_op jit(solution)/shard_map/all_gather | solution.py:190
  83.2 2.0 copy-start.2
  85.8 5.0 %collective-permute-start = (f32[8,128,128]{2,1,0:T(8,128)S(1)}, f32[8,128,128]{2,1,0:T(8,128)}, u32[]{:S(2)}, u32[]{:S(2)}) collective-permute-start(f32[8,128,128]{2,1,0:T(8,128)S(1)} %fusion.26), channel_id=1, source_target_pairs={{0,2},{2,4},{4,6},{6,8},{8,10},{10,12},{12,14},{14,16},{16,18},{18... | collective-permute-start | bytes 1572872 | tf_op jit(solution)/shard_map/ppermute | solution.py:49
  91.9 17.2 %collective-permute-start.1 = (f32[8,128,128]{2,1,0:T(8,128)S(1)}, f32[8,128,128]{2,1,0:T(8,128)S(1)}, u32[]{:S(2)}, u32[]{:S(2)}) collective-permute-start(f32[8,128,128]{2,1,0:T(8,128)S(1)} %broadcast_select_fusion), channel_id=1, source_target_pairs={{0,2},{2,4},{4,6},{6,8},{8,10},{10,12},{12,14},{14,16},{16,18},{18... | collective-permute-start | bytes 1572872 | tf_op jit(solution)/shard_map/ppermute | solution.py:53
  109.7 14.6 %collective-permute-start.2 = (f32[8,128,128]{2,1,0:T(8,128)S(1)}, f32[8,128,128]{2,1,0:T(8,128)}, u32[]{:S(2)}, u32[]{:S(2)}) collective-permute-start(f32[8,128,128]{2,1,0:T(8,128)S(1)} %convolution_select_fusion.6), channel_id=1, source_target_pairs={{0,4},{2,6},{4,8},{6,10},{8,12},{10,14},{12,16},{14,18},{16,20},{1... | collective-permute-start | bytes 1572872 | tf_op jit(solution)/shard_map/ppermute | solution.py:53
  126.1 23.2 %collective-permute-start.3 = (f32[8,128,128]{2,1,0:T(8,128)S(1)}, f32[8,128,128]{2,1,0:T(8,128)S(1)}, u32[]{:S(2)}, u32[]{:S(2)}) collective-permute-start(f32[8,128,128]{2,1,0:T(8,128)S(1)} %convolution_select_fusion.5), channel_id=1, source_target_pairs={{0,8},{2,10},{4,12},{6,14},{8,16},{10,18},{12,20},{14,22},{16,24},... | collective-permute-start | bytes 1572872 | tf_op jit(solution)/shard_map/ppermute | solution.py:53
  128.3 24.3 %copy-start.3 = (f32[8,8,128,128]{3,2,1,0:T(8,128)S(1)}, f32[8,8,128,128]{3,2,1,0:T(8,128)}, u32[]{:S(2)}) copy-start(f32[8,8,128,128]{3,2,1,0:T(8,128)} %copy-done.2) | copy-start | bytes 12582916
  149.9 26.9 %collective-permute-start.4 = (f32[8,128,128]{2,1,0:T(8,128)S(1)}, f32[8,128,128]{2,1,0:T(8,128)S(1)}, u32[]{:S(2)}, u32[]{:S(2)}) collective-permute-start(f32[8,128,128]{2,1,0:T(8,128)S(1)} %convolution_select_fusion.4), channel_id=1, source_target_pairs={{0,16},{2,18},{4,20},{6,22},{8,24},{10,26},{12,28},{14,30},{1,17},... | collective-permute-start | bytes 1572872 | tf_op jit(solution)/shard_map/ppermute | solution.py:53
  181.4 173.4 %reduce-scatter.2.cloned.1.call-start = ((), (), s32[]{:S(2)}) async-start(), calls=%async_computation.3 | async-start | bytes 3145728 | tf_op jit(solution)/shard_map/reduce_scatter | solution.py:194
  181.8 4.0 %copy-start.4 = (f32[8,8,128,128]{3,2,1,0:T(8,128)S(1)}, f32[8,8,128,128]{3,2,1,0:T(8,128)}, u32[]{:S(2)}) copy-start(f32[8,8,128,128]{3,2,1,0:T(8,128)} %copy-done.2) | copy-start | bytes 12582916
  315.2 39.7 %copy-start.1 = (bf16[1024,1024]{1,0:T(8,128)(2,1)S(1)}, bf16[1024,1024]{1,0:T(8,128)(2,1)}, u32[]{:S(2)}) copy-start(bf16[1024,1024]{1,0:T(8,128)(2,1)} %param.10) | copy-start | bytes 6291460
Sparse Core Ops, SparseCore 0:
  40.1 78.2 all-gather.5
  181.6 74.6 all-gather.3
  322.7 32.1 reduce-scatter.1
where the time goes:
time: 367 us; the launch traced here: 362 us
  waiting for transfers between devices  162 us (44%)
  matrix products  76.9 us (21%)
  Pallas kernels  58.9 us (16%)
  blocking collectives  22.3 us (6%)
  local copies, waits for them, and re-layouts  16.3 us (4%)
  between operations  14.1 us (4%)
  starting transfers between devices  7.01 us (2%)
  other arithmetic  4.25 us (1%)
    ppermute x4, waiting for transfers between devices, exclusive_shards(): lax.ppermute(acc, axis, [(i, i + shift) for i in range(length - shift)])  64.6 us
    all_gather x1, waiting for transfers between devices, local(): k_all = lax.all_gather(k_glob, 'ctx', axis=0, tiled=True)  61.6 us
    pallas_call x1, Pallas kernels, flash_attend(): pl.pallas_call(kernel, grid_spec=grid_spec, out_shape=jax.ShapeDtypeStruc...  58.9 us
    dot_general x20, matrix products, mm(): return jnp.einsum('...ij,...jk->...ik', a, b, precision=HP)  32.9 us
    reduce_scatter x1, waiting for transfers between devices, local(): lax.psum_scatter(jnp.dot(attn, out_weight, preferred_element_type=jnp.flo...  32.3 us
    all_to_all x1, blocking collectives, local(): lax.all_to_all(stacked, 'hg', split_axis=2, concat_axis=0, tiled=True)  22.3 us
    dot_general x2, matrix products, in_shard(): moved = jnp.einsum('hnid,hned->hnie', inblock, inner_prefix, precision=HP)  13.5 us
    unnamed x17, local copies, waits for them, and re-layouts  8.02 us
  transfers between devices with their start and end apart: 8, of which 7 were waited for; matrix products, arithmetic and copies ran while one was open for 21% of the time, Pallas kernels for 0%

commit v1 on v0

--- a/solution.py
+++ b/solution.py
@@ -56,9 +56,9 @@
     return acc
 
 
-def flash_attend(q_glob, k_all, v_all, shard, heads):
+def flash_attend(q_glob, kt_all, v_all, part, shard, heads):
     rows, width = q_glob.shape
-    nk = k_all.shape[0] // rows
+    nk = kt_all.shape[0]
     scale = 1.0 / math.sqrt(HDIM)
 
     def kernel(c_ref, q_ref, k_ref, v_ref, o_ref, m_sc, l_sc, acc_sc):
@@ -75,14 +75,9 @@
             for hh in range(heads):
                 sl = slice(hh * HDIM, (hh + 1) * HDIM)
                 qh = q_ref[:, sl]
-                kh = k_ref[:, sl]
+                kh = k_ref[sl, :]
                 vh = v_ref[:, sl]
-                s = (
-                    lax.dot_general(
-                        qh, kh, (((1,), (1,)), ((), ())), preferred_element_type=jnp.float32
-                    )
-                    * scale
-                )
+                s = jnp.dot(qh, kh, preferred_element_type=jnp.float32) * scale
                 if masked:
                     row = lax.broadcasted_iota(jnp.int32, s.shape, 0)
                     col = lax.broadcasted_iota(jnp.int32, s.shape, 1)
@@ -119,8 +114,8 @@
         grid=(nk,),
         in_specs=[
             pl.BlockSpec((rows, width), lambda j, c: (0, 0)),
-            pl.BlockSpec((rows, width), lambda j, c: (jnp.minimum(j, c[0]), 0)),
-            pl.BlockSpec((rows, width), lambda j, c: (jnp.minimum(j, c[0]), 0)),
+            pl.BlockSpec((None, width, rows), lambda j, c: (jnp.minimum(j, c[0]), 0, 0)),
+            pl.BlockSpec((None, rows, width), lambda j, c: (jnp.minimum(j, c[0]), 0, part)),
         ],
         out_specs=pl.BlockSpec((rows, width), lambda j, c: (0, 0)),
         scratch_shapes=[
@@ -134,7 +129,39 @@
         grid_spec=grid_spec,
         out_shape=jax.ShapeDtypeStruct((rows, width), jnp.bfloat16),
         compiler_params=pltpu.CompilerParams(dimension_semantics=("arbitrary",)),
-    )(jnp.reshape(shard, (1,)).astype(jnp.int32), q_glob, k_all, v_all)
+    )(jnp.reshape(shard, (1,)).astype(jnp.int32), q_glob, kt_all, v_all)
+
+
+SWAP = [(0, 1), (1, 0)]
+
+
+def exchange_heads(stacked, groups):
+    if groups != 2:
+        return lax.all_to_all(stacked, "hg", split_axis=2, concat_axis=0, tiled=True)[:, :, 0]
+    first = lax.axis_index("hg") == 0
+    own = jnp.where(first, stacked[:, :, 0], stacked[:, :, 1])
+    got = lax.ppermute(jnp.where(first, stacked[:, :, 1], stacked[:, :, 0]), "hg", SWAP)
+    return jnp.where(
+        first, jnp.concatenate([own, got], axis=0), jnp.concatenate([got, own], axis=0)
+    )
+
+
+def project_out(attn, out_weight, groups):
+    if groups != 2:
+        return lax.psum_scatter(
+            jnp.dot(attn, out_weight, preferred_element_type=jnp.float32).astype(jnp.bfloat16),
+            "hg",
+            scatter_dimension=0,
+            tiled=True,
+        )
+    half = attn.shape[0] // 2
+    first = lax.axis_index("hg") == 0
+    theirs = jnp.where(first, attn[half:], attn[:half])
+    mine = jnp.where(first, attn[:half], attn[half:])
+    sent = jnp.dot(theirs, out_weight, preferred_element_type=jnp.float32).astype(jnp.bfloat16)
+    got = lax.ppermute(sent, "hg", SWAP)
+    kept = jnp.dot(mine, out_weight, preferred_element_type=jnp.float32)
+    return (kept + got.astype(jnp.float32)).astype(jnp.bfloat16)
 
 
 def local(queries, keys, values, reflect_ids, reflect_bank, out_weight):
@@ -144,12 +171,12 @@
     stacked = jnp.stack([queries, keys, values], axis=1).reshape(
         queries.shape[0], 3, groups, width
     )
-    swapped = lax.all_to_all(stacked, "hg", split_axis=2, concat_axis=0, tiled=True)
+    swapped, reflect_ids = lax.optimization_barrier((exchange_heads(stacked, groups), reflect_ids))
     rows = swapped.shape[0]
-    q_local = swapped[:, 0, 0]
-    k_local = swapped[:, 1, 0]
-    v_local = swapped[:, 2, 0]
-    v_all = lax.all_gather(v_local, "ctx", axis=0, tiled=True)
+    q_local = swapped[:, 0]
+    k_local = swapped[:, 1]
+    v_local = swapped[:, 2]
+    v_all = lax.all_gather(v_local, "ctx", axis=0, tiled=False)
 
     nblocks = rows // BLK
     bank = reflect_bank.shape[0]
@@ -171,7 +198,7 @@
     lower_mask = jnp.tril(jnp.ones((BLK, BLK), dtype=jnp.bool_))
 
     inner_prefix, shard_prod = exclusive_blocks(block_mats)
-    earlier_prod = exclusive_shards(shard_prod, "ctx")
+    earlier_prod, v_all = lax.optimization_barrier((exclusive_shards(shard_prod, "ctx"), v_all))
 
     def in_shard(matrix):
         split = matrix.astype(jnp.float32).reshape(nblocks, BLK, heads, HDIM).transpose(2, 0, 1, 3)
@@ -182,21 +209,30 @@
         moved = jnp.einsum("hnid,hned->hnie", inblock, inner_prefix, precision=HP)
         return moved.reshape(heads, rows, HDIM)
 
-    def to_global(moved):
-        full = jnp.einsum("hie,hfe->hif", moved, earlier_prod, precision=HP)
-        return full.transpose(1, 0, 2).reshape(rows, width).astype(jnp.bfloat16)
-
-    k_glob = to_global(in_shard(k_local))
-    k_all = lax.all_gather(k_glob, "ctx", axis=0, tiled=True)
-    q_glob = to_global(in_shard(q_local))
-
-    attn = flash_attend(q_glob, k_all, v_all, lax.axis_index("ctx"), heads)
-    return lax.psum_scatter(
-        jnp.dot(attn, out_weight, preferred_element_type=jnp.float32).astype(jnp.bfloat16),
-        "hg",
-        scatter_dimension=0,
-        tiled=True,
-    )
+    kt_glob = jnp.einsum(
+        "hie,hfe->hfi", in_shard(k_local), earlier_prod, precision=HP
+    ).reshape(width, rows).astype(jnp.bfloat16)
+    parts = 2 if heads % 2 == 0 else 1
+    pw = width // parts
+    kt_parts = [
+        lax.all_gather(kt_glob[p * pw : (p + 1) * pw], "ctx", axis=0, tiled=False)
+        for p in range(parts)
+    ]
+    q_glob = (
+        jnp.einsum("hie,hfe->hif", in_shard(q_local), earlier_prod, precision=HP)
+        .transpose(1, 0, 2)
+        .reshape(rows, width)
+        .astype(jnp.bfloat16)
+    )
+    shard = lax.axis_index("ctx")
+    attn = jnp.concatenate(
+        [
+            flash_attend(q_glob[:, p * pw : (p + 1) * pw], kt_parts[p], v_all, p, shard, heads // parts)
+            for p in range(parts)
+        ],
+        axis=1,
+    )
+    return project_out(attn, out_weight, groups)
 
 
 def solution(mesh):

time: 367 us -> 357 us (0.973)
  blocking collectives: 22.3 us -> 0 us
  Pallas kernels: 58.9 us -> 66.8 us
  matrix products: 76.9 us -> 81.5 us
    ppermute x0 -> x2, waiting for transfers between devices: none -> 39.7 us  [the longest x1 22.5 us: project_out(): got = lax.ppermute(sent, 'hg', SWAP)]
    reduce_scatter x1 -> x0, waiting for transfers between devices: 32.3 us -> none  [local(): lax.psum_scatter(jnp.dot(attn, out_weight, preferred_element_type=jnp.flo...]
    all_to_all x1 -> x0, blocking collectives: 22.3 us -> none  [local(): lax.all_to_all(stacked, 'hg', split_axis=2, concat_axis=0, tiled=True)]
    pallas_call x1 -> x2, Pallas kernels: 58.9 us -> 66.8 us  [flash_attend(): pl.pallas_call(kernel, grid_spec=grid_spec, out_shape=jax.ShapeDtypeStruc...]
    all_gather x2 -> x3, waiting for transfers between devices: 61.6 us -> 53.8 us  [the longest x2 53.8 us: local(): lax.all_gather(kt_glob[p * pw:(p + 1) * pw], 'ctx', axis=0, tiled=False)]
    dot_general x3 -> x4, matrix products: 10.3 us -> 14 us  [the longest x1 5.81 us: project_out(): kept = jnp.dot(mine, out_weight, preferred_element_type=jnp.float32)]
    unnamed x17 -> x23, local copies, waits for them, and re-layouts: 8.02 us -> 7.93 us
  transfers between devices with their start and end apart: 8 -> 10, of which waited for: 7 -> 9; matrix products, arithmetic and copies ran while one was open for 21% -> 21% of each run, Pallas kernels for 0% -> 9%
where the time goes in v1:
time: 357 us; the launch traced here: 354 us
  waiting for transfers between devices  162 us (45%)
  matrix products  81.5 us (23%)
  Pallas kernels  66.8 us (19%)
  local copies, waits for them, and re-layouts  15.5 us (4%)
  between operations  13.8 us (4%)
  starting transfers between devices  9.73 us (3%)
  other arithmetic  4.03 us (1%)
    pallas_call x2, Pallas kernels, flash_attend(): pl.pallas_call(kernel, grid_spec=grid_spec, out_shape=jax.ShapeDtypeStruc...  66.8 us
    ppermute x4, waiting for transfers between devices, exclusive_shards(): lax.ppermute(acc, axis, [(i, i + shift) for i in range(length - shift)])  64.8 us
    all_gather x2, waiting for transfers between devices, local(): lax.all_gather(kt_glob[p * pw:(p + 1) * pw], 'ctx', axis=0, tiled=False)  53.8 us
    dot_general x20, matrix products, mm(): return jnp.einsum('...ij,...jk->...ik', a, b, precision=HP)  32.9 us
    ppermute x1, waiting for transfers between devices, project_out(): got = lax.ppermute(sent, 'hg', SWAP)  22.5 us
    ppermute x1, waiting for transfers between devices, exchange_heads(): lax.ppermute(jnp.where(first, stacked[:, :, 1], stacked[:, :, 0]), 'hg',...  17.2 us
    dot_general x2, matrix products, in_shard(): moved = jnp.einsum('hnid,hned->hnie', inblock, inner_prefix, precision=HP)  14.5 us
    unnamed x23, local copies, waits for them, and re-layouts  7.93 us
  transfers between devices with their start and end apart: 10, of which 9 were waited for; matrix products, arithmetic and copies ran while one was open for 21% of the time, Pallas kernels for 9%

profile of v1, /device:TPU:27, one launch (start us, length us, event | category | flops | bytes accessed | tf_op | source)
XLA Modules:
  0.0 353.6 jit_solution(4230629250405242406)
XLA Ops:
  6.5 1.6 stack.12
  9.1 1.4 stack.13
  10.5 1.4 stack.14
  13.8 1.5 select_bitcast_fusion.1
  15.2 1.3 collective-permute-start
  16.5 17.2 %collective-permute-done = bf16[128,3,1024]{2,0,1:T(8,128)(2,1)S(1)} collective-permute-done((bf16[128,3,1024]{2,0,1:T(8,128)(2,1)S(1)}, bf16[128,3,1024]{2,0,1:T(8,128)(2,1)S(1)}, u32[]{:S(2)}, u32[]{:S(2)}) %collective-permute-start) | collective-permute-done | bytes 786464 | tf_op jit(solution)/shard_map/ppermute | solution.py:143
  35.7 2.2 multiply_reduce_fusion
  38.2 1.8 fusion.14
  40.0 1.2 fusion.55
  41.2 1.2 fusion.56
  42.4 1.2 fusion.57
  43.6 1.2 fusion.58
  44.8 1.2 fusion.59
  46.0 1.2 fusion.23
  47.2 1.2 fusion.21
  48.4 1.2 fusion.19
  49.6 1.4 fusion.17
  55.6 7.1 %convolution_subtract_fusion = f32[8,8,128,128]{3,2,1,0:T(8,128)S(1)} fusion(f32[8,8,32,128]{3,2,1,0:T(8,128)S(1)} %bitcast.111, f32[8,8,32,128]{3,2,1,0:T(8,128)S(1)} %fusion.61, f32[128,128]{1,0:T(8,128)S(1)} %fusion.44), kind=kOutput, calls=%fused_computation.19 | convolution fusion | flops 403701760 | bytes 6356992 | tf_op jit(solution)/shard_map/hnkd,hnke->hnde/dot_general | solution.py:197
  63.6 4.7 %fusion.1 = f32[8,8,128,128]{3,2,1,0:T(8,128)S(1)} fusion(f32[8,1,128,128]{3,2,1,0:T(8,128)S(1)} %broadcast_in_dim.41, f32[8,7,128,128]{3,2,1,0:T(8,128)S(1)} %slice.76, f32[8,7,128,128]{3,2,1,0:T(8,128)S(1)} %fusion.12), kind=kOutput, calls=%fused_computation.7 | convolution fusion | flops 1612709888 | bytes 12058624 | tf_op jit(solution)/shard_map/...ij,...jk->...ik/dot_general | solution.py:16
  68.8 4.7 %fusion.3 = f32[8,8,128,128]{3,2,1,0:T(8,128)S(1)} fusion(f32[8,8,128,128]{3,2,1,0:T(8,128)S(1)} %fusion.1, f32[8,6,128,128]{3,2,1,0:T(8,128)S(1)} %slice.79, f32[8,2,128,128]{3,2,1,0:T(8,128)S(1)} %broadcast_in_dim_broadcast_in_dim.7), kind=kOutput, calls=%fused_computation.9 | convolution fusion | flops 1611661312 | bytes 12582912 | tf_op jit(solution)/shard_map/...ij,...jk->...ik/dot_general | solution.py:16
  73.9 4.9 %fusion.7 = f32[8,8,128,128]{3,2,1,0:T(8,128)S(1)} fusion(f32[8,8,128,128]{3,2,1,0:T(8,128)S(1)} %fusion.3, f32[8,4,128,128]{3,2,1,0:T(8,128)S(1)} %slice.80, f32[8,4,128,128]{3,2,1,0:T(8,128)S(1)} %broadcast_in_dim_broadcast_in_dim.6), kind=kOutput, calls=%fused_computation.13 | convolution fusion | flops 1611661312 | bytes 12582912 | tf_op jit(solution)/shard_map/...ij,...jk->...ik/dot_general | solution.py:16
  78.8 2.0 copy-done.2
  81.5 1.3 collective-permute-start.1
  82.8 3.7 %collective-permute-done.1 = f32[8,128,128]{2,1,0:T(8,128)} collective-permute-done((f32[8,128,128]{2,1,0:T(8,128)S(1)}, f32[8,128,128]{2,1,0:T(8,128)}, u32[]{:S(2)}, u32[]{:S(2)}) %collective-permute-start.1) | collective-permute-done | bytes 524320 | tf_op jit(solution)/shard_map/ppermute | solution.py:49
  87.5 1.3 collective-permute-start.2
  88.8 16.9 %collective-permute-done.2 = f32[8,128,128]{2,1,0:T(8,128)S(1)} collective-permute-done((f32[8,128,128]{2,1,0:T(8,128)S(1)}, f32[8,128,128]{2,1,0:T(8,128)S(1)}, u32[]{:S(2)}, u32[]{:S(2)}) %collective-permute-start.2) | collective-permute-done | bytes 524320 | tf_op jit(solution)/shard_map/ppermute | solution.py:53
  106.3 1.3 collective-permute-start.3
  108.8 12.2 %collective-permute-done.3 = f32[8,128,128]{2,1,0:T(8,128)} collective-permute-done((f32[8,128,128]{2,1,0:T(8,128)S(1)}, f32[8,128,128]{2,1,0:T(8,128)}, u32[]{:S(2)}, u32[]{:S(2)}) %collective-permute-start.3) | collective-permute-done | bytes 524320 | tf_op jit(solution)/shard_map/ppermute | solution.py:53
  121.0 1.7 convolution_select_fusion.5
  122.7 1.3 collective-permute-start.4
  124.9 1.8 fusion.63
  126.7 19.3 %collective-permute-done.4 = f32[8,128,128]{2,1,0:T(8,128)S(1)} collective-permute-done((f32[8,128,128]{2,1,0:T(8,128)S(1)}, f32[8,128,128]{2,1,0:T(8,128)S(1)}, u32[]{:S(2)}, u32[]{:S(2)}) %collective-permute-start.4) | collective-permute-done | bytes 524320 | tf_op jit(solution)/shard_map/ppermute | solution.py:53
  146.7 1.5 collective-permute-start.5
  148.2 1.2 convolution_subtract_fusion.1
  149.5 7.7 %fusion.64 = f32[8,8,32,128]{3,2,1,0:T(8,128)} fusion(f32[8,8,32,128]{3,2,1,0:T(8,128)S(1)} %convolution_subtract_fusion.1, f32[8,8,128,128]{3,2,1,0:T(8,128)S(1)} %copy-done.3), kind=kOutput, calls=%fused_computation.102 | convolution fusion | flops 402653184 | bytes 6291456 | tf_op jit(solution)/shard_map/hnid,hned->hnie/dot_general | solution.py:209
  157.2 16.4 %collective-permute-done.5 = f32[8,128,128]{2,1,0:T(8,128)S(1)} collective-permute-done((f32[8,128,128]{2,1,0:T(8,128)S(1)}, f32[8,128,128]{2,1,0:T(8,128)S(1)}, u32[]{:S(2)}, u32[]{:S(2)}) %collective-permute-start.5) | collective-permute-done | bytes 524320 | tf_op jit(solution)/shard_map/ppermute | solution.py:53
  174.3 2.3 convolution_convert_fusion.1
  179.2 1.8 fusion.60
  181.0 1.2 convolution_subtract_fusion.2
  182.3 6.8 %fusion.62 = f32[8,8,32,128]{3,2,1,0:T(8,128)S(1)} fusion(f32[8,8,32,128]{3,2,1,0:T(8,128)S(1)} %convolution_subtract_fusion.2, f32[8,8,128,128]{3,2,1,0:T(8,128)S(1)} %copy-done.4), kind=kOutput, calls=%fused_computation.100 | convolution fusion | flops 402653184 | bytes 6291456 | tf_op jit(solution)/shard_map/hnid,hned->hnie/dot_general | solution.py:209
  191.8 36.0 %all-gather.7.cloned.1.call-done.k_ref = bf16[16,512,256]{2,1,0:T(8,128)(2,1)} async-done(((bf16[1,512,256]{2,1,0:T(8,128)(2,1)}), bf16[16,512,256]{2,1,0:T(8,128)(2,1)}) %all-gather.7.cloned.1.call-update) | async-done | bytes 4194320 | tf_op jit(solution)/shard_map/all_gather | solution.py:218
  227.9 33.5 %shard_map.65 = bf16[256,512]{1,0:T(8,128)(2,1)} custom-call(s32[1]{0:T(128)} %bitcast.c_ref, bf16[256,512]{1,0:T(8,128)(2,1)} %copy.28.q_ref, bf16[16,512,256]{2,1,0:T(8,128)(2,1)} %all-gather.7.cloned.1.call-done.k_ref, bf16[16,256,1024]{2,1,0:T(8,128)(2,1)} %bitcast.116), custom_call_target="tpu_custom_call" | custom-call | tf_op jit(solution)/shard_map/pallas_call | solution.py:127
  261.4 17.8 %all-gather.5.cloned.1.call-done.k_ref = bf16[16,512,256]{2,1,0:T(8,128)(2,1)} async-done(((bf16[1,512,256]{2,1,0:T(8,128)(2,1)}), bf16[16,512,256]{2,1,0:T(8,128)(2,1)}) %all-gather.5.cloned.1.call-update) | async-done | bytes 4194320 | tf_op jit(solution)/shard_map/all_gather | solution.py:218
  279.1 33.3 %shard_map.64 = bf16[256,512]{1,0:T(8,128)(2,1)} custom-call(s32[1]{0:T(128)} %bitcast.c_ref, bf16[256,512]{1,0:T(8,128)(2,1)} %copy.27.q_ref, bf16[16,512,256]{2,1,0:T(8,128)(2,1)} %all-gather.5.cloned.1.call-done.k_ref, bf16[16,256,1024]{2,1,0:T(8,128)(2,1)} %bitcast.117), custom_call_target="tpu_custom_call" | custom-call | tf_op jit(solution)/shard_map/pallas_call | solution.py:127
  312.4 4.8 %convolution_convert_fusion = bf16[128,4096]{1,0:T(8,128)(2,1)S(1)} fusion(bf16[1024,4096]{1,0:T(8,128)(2,1)} %param.11, pred[]{:T(512)S(6)} %eq.55, bf16[256,512]{1,0:T(8,128)(2,1)S(1)} %copy-done.5, bf16[256,512]{1,0:T(8,128)(2,1)} %shard_map.64), kind=kOutput, calls=%fused_computation.5 | convolution fusion | flops 1075445760 | bytes 9961473 | tf_op jit(solution)/shard_map/dot_general | solution.py:161
  317.3 1.3 collective-permute-start.6
  318.5 22.5 %collective-permute-done.6 = bf16[128,4096]{1,0:T(8,128)(2,1)S(1)} collective-permute-done((bf16[128,4096]{1,0:T(8,128)(2,1)S(1)}, bf16[128,4096]{1,0:T(8,128)(2,1)S(1)}, u32[]{:S(2)}, u32[]{:S(2)}) %collective-permute-start.6) | collective-permute-done | bytes 1048608 | tf_op jit(solution)/shard_map/ppermute | solution.py:162
  341.0 5.8 %add_convert_fusion = bf16[128,4096]{1,0:T(8,128)(2,1)} fusion(bf16[128,4096]{1,0:T(8,128)(2,1)S(1)} %collective-permute-done.6, bf16[1024,4096]{1,0:T(8,128)(2,1)} %param.11, pred[]{:T(512)S(6)} %eq.55, bf16[256,512]{1,0:T(8,128)(2,1)S(1)} %copy-done.5, bf16[256,512]{1,0:T(8,128)(2,1)S(1)} %copy-done.6), kind=kOutput, calls=%fused_computation.22 | convolution fusion | flops 1076494336 | bytes 11010049 | tf_op jit(solution)/shard_map/dot_general | solution.py:163
  (57 shorter events, 22.7 us)
Async XLA Ops:
  6.5 29.2 %copy-start = (bf16[1024,1024]{1,0:T(8,128)(2,1)S(1)}, bf16[1024,1024]{1,0:T(8,128)(2,1)}, u32[]{:S(2)}) copy-start(bf16[1024,1024]{1,0:T(8,128)(2,1)} %param.10) | copy-start | bytes 6291460
  6.5 167.8 %all-gather.9.cloned.1.call-start = ((), (), s32[]{:S(2)}) async-start(), calls=%async_computation.2 | async-start | bytes 8912896 | tf_op jit(solution)/shard_map/all_gather | solution.py:179
  15.2 20.5 %copy-start.7 = (s32[256,8]{0,1:T(8,128)S(1)}, s32[256,8]{0,1:T(8,128)}, u32[]{:S(2)}) copy-start(s32[256,8]{0,1:T(8,128)} %param.9) | copy-start | bytes 24580
  15.2 18.5 %collective-permute-start = (bf16[128,3,1024]{2,0,1:T(8,128)(2,1)S(1)}, bf16[128,3,1024]{2,0,1:T(8,128)(2,1)S(1)}, u32[]{:S(2)}, u32[]{:S(2)}) collective-permute-start(bf16[128,3,1024]{2,0,1:T(8,128)(2,1)S(1)} %get-tuple-element.17), channel_id=1, source_target_pairs={{0,1},{1,0},{2,3},{3,2},{4,5},{5,4},{6,7},{7,6},{8,9},{9,8},{10,11... | collective-permute-start | bytes 2359304 | tf_op jit(solution)/shard_map/ppermute | solution.py:143
  35.6 192.3 %all-gather.7.cloned.1.call-start = ((), (), s32[]{:S(2)}) async-start(), calls=%async_computation.1 | async-start | bytes 4456448 | tf_op jit(solution)/shard_map/all_gather | solution.py:218
  78.8 2.0 copy-start.2
  81.5 5.0 %collective-permute-start.1 = (f32[8,128,128]{2,1,0:T(8,128)S(1)}, f32[8,128,128]{2,1,0:T(8,128)}, u32[]{:S(2)}, u32[]{:S(2)}) collective-permute-start(f32[8,128,128]{2,1,0:T(8,128)S(1)} %fusion.26), channel_id=1, source_target_pairs={{0,2},{2,4},{4,6},{6,8},{8,10},{10,12},{12,14},{14,16},{16,18},{18... | collective-permute-start | bytes 1572872 | tf_op jit(solution)/shard_map/ppermute | solution.py:49
  87.5 18.2 %collective-permute-start.2 = (f32[8,128,128]{2,1,0:T(8,128)S(1)}, f32[8,128,128]{2,1,0:T(8,128)S(1)}, u32[]{:S(2)}, u32[]{:S(2)}) collective-permute-start(f32[8,128,128]{2,1,0:T(8,128)S(1)} %broadcast_select_fusion), channel_id=1, source_target_pairs={{0,2},{2,4},{4,6},{6,8},{8,10},{10,12},{12,14},{14,16},{16,18},{18... | collective-permute-start | bytes 1572872 | tf_op jit(solution)/shard_map/ppermute | solution.py:53
  106.3 14.6 %collective-permute-start.3 = (f32[8,128,128]{2,1,0:T(8,128)S(1)}, f32[8,128,128]{2,1,0:T(8,128)}, u32[]{:S(2)}, u32[]{:S(2)}) collective-permute-start(f32[8,128,128]{2,1,0:T(8,128)S(1)} %convolution_select_fusion.6), channel_id=1, source_target_pairs={{0,4},{2,6},{4,8},{6,10},{8,12},{10,14},{12,16},{14,18},{16,20},{1... | collective-permute-start | bytes 1572872 | tf_op jit(solution)/shard_map/ppermute | solution.py:53
  122.7 23.4 %collective-permute-start.4 = (f32[8,128,128]{2,1,0:T(8,128)S(1)}, f32[8,128,128]{2,1,0:T(8,128)S(1)}, u32[]{:S(2)}, u32[]{:S(2)}) collective-permute-start(f32[8,128,128]{2,1,0:T(8,128)S(1)} %convolution_select_fusion.5), channel_id=1, source_target_pairs={{0,8},{2,10},{4,12},{6,14},{8,16},{10,18},{12,20},{14,22},{16,24},... | collective-permute-start | bytes 1572872 | tf_op jit(solution)/shard_map/ppermute | solution.py:53
  124.9 24.5 %copy-start.3 = (f32[8,8,128,128]{3,2,1,0:T(8,128)S(1)}, f32[8,8,128,128]{3,2,1,0:T(8,128)}, u32[]{:S(2)}) copy-start(f32[8,8,128,128]{3,2,1,0:T(8,128)} %copy-done.2) | copy-start | bytes 12582916
  146.7 26.9 %collective-permute-start.5 = (f32[8,128,128]{2,1,0:T(8,128)S(1)}, f32[8,128,128]{2,1,0:T(8,128)S(1)}, u32[]{:S(2)}, u32[]{:S(2)}) collective-permute-start(f32[8,128,128]{2,1,0:T(8,128)S(1)} %convolution_select_fusion.4), channel_id=1, source_target_pairs={{0,16},{2,18},{4,20},{6,22},{8,24},{10,26},{12,28},{14,30},{1,17},... | collective-permute-start | bytes 1572872 | tf_op jit(solution)/shard_map/ppermute | solution.py:53
  177.4 101.7 %all-gather.5.cloned.1.call-start = ((), (), s32[]{:S(2)}) async-start(), calls=%async_computation | async-start | bytes 4456448 | tf_op jit(solution)/shard_map/all_gather | solution.py:218
  179.2 3.0 copy-start.4
  261.4 51.1 %copy-start.5 = (bf16[256,512]{1,0:T(8,128)(2,1)S(1)}, bf16[256,512]{1,0:T(8,128)(2,1)}, u32[]{:S(2)}) copy-start(bf16[256,512]{1,0:T(8,128)(2,1)} %shard_map.65) | copy-start | bytes 786436
  312.4 28.6 %copy-start.6 = (bf16[256,512]{1,0:T(8,128)(2,1)S(1)}, bf16[256,512]{1,0:T(8,128)(2,1)}, u32[]{:S(2)}) copy-start(bf16[256,512]{1,0:T(8,128)(2,1)} %shard_map.64) | copy-start | bytes 786436
  317.3 23.8 %collective-permute-start.6 = (bf16[128,4096]{1,0:T(8,128)(2,1)S(1)}, bf16[128,4096]{1,0:T(8,128)(2,1)S(1)}, u32[]{:S(2)}, u32[]{:S(2)}) collective-permute-start(bf16[128,4096]{1,0:T(8,128)(2,1)S(1)} %convolution_convert_fusion), channel_id=1, source_target_pairs={{0,1},{1,0},{2,3},{3,2},{4,5},{5,4},{6,7},{7,6},{8,9},{9,8},{10,11... | collective-permute-start | bytes 3145736 | tf_op jit(solution)/shard_map/ppermute | solution.py:162
  341.0 5.8 %copy-start.1 = (bf16[1024,1024]{1,0:T(8,128)(2,1)S(1)}, bf16[1024,1024]{1,0:T(8,128)(2,1)}, u32[]{:S(2)}) copy-start(bf16[1024,1024]{1,0:T(8,128)(2,1)} %param.10) | copy-start | bytes 6291460
Sparse Core Ops, SparseCore 0:
  35.7 79.5 all-gather.8
  177.6 50.2 all-gather.6
  230.0 49.0 all-gather.4

commit v2 on v1

--- a/solution.py
+++ b/solution.py
@@ -9,6 +9,7 @@
 
 HDIM = 128
 BLK = 32
+GROUP = 1
 HP = lax.Precision.HIGHEST
 
 
@@ -56,9 +57,12 @@
     return acc
 
 
-def flash_attend(q_glob, kt_all, v_all, part, shard, heads):
+def flash_attend(q_glob, kt_all, v_all, part, shard, heads, group=GROUP):
     rows, width = q_glob.shape
     nk = kt_all.shape[0]
+    while nk % group:
+        group //= 2
+    nb = nk // group
     scale = 1.0 / math.sqrt(HDIM)
 
     def kernel(c_ref, q_ref, k_ref, v_ref, o_ref, m_sc, l_sc, acc_sc):
@@ -71,12 +75,12 @@
             l_sc[...] = jnp.zeros(l_sc.shape, jnp.float32)
             acc_sc[...] = jnp.zeros(acc_sc.shape, jnp.float32)
 
-        def step(masked):
+        def step(g, masked):
             for hh in range(heads):
                 sl = slice(hh * HDIM, (hh + 1) * HDIM)
                 qh = q_ref[:, sl]
-                kh = k_ref[sl, :]
-                vh = v_ref[:, sl]
+                kh = k_ref[g, sl, :]
+                vh = v_ref[g, :, sl]
                 s = jnp.dot(qh, kh, preferred_element_type=jnp.float32) * scale
                 if masked:
                     row = lax.broadcasted_iota(jnp.int32, s.shape, 0)
@@ -85,7 +89,11 @@
                     s = jnp.where(allowed, s, -1e30)
                 m_prev = m_sc[hh]
                 m_new = jnp.maximum(m_prev, jnp.max(s, axis=1, keepdims=True))
-                p = jnp.exp(s - m_new)
+                if s.shape[1] % HDIM == 0:
+                    wide = jnp.concatenate([m_new] * (s.shape[1] // HDIM), axis=1)
+                else:
+                    wide = m_new[:, :1]
+                p = jnp.exp(s - wide)
                 if masked:
                     p = jnp.where(allowed, p, 0.0)
                 fade = jnp.exp(m_prev - m_new)
@@ -95,15 +103,18 @@
                 )
                 m_sc[hh] = m_new
 
-        @pl.when(j < c)
-        def _():
-            step(False)
-
-        @pl.when(j == c)
-        def _():
-            step(True)
-
-        @pl.when(j == nk - 1)
+        for g in range(group):
+            here = j * group + g
+
+            @pl.when(here < c)
+            def _():
+                step(g, False)
+
+            @pl.when(here == c)
+            def _():
+                step(g, True)
+
+        @pl.when(j == nb - 1)
         def _():
             for hh in range(heads):
                 sl = slice(hh * HDIM, (hh + 1) * HDIM)
@@ -111,16 +122,16 @@
 
     grid_spec = pltpu.PrefetchScalarGridSpec(
         num_scalar_prefetch=1,
-        grid=(nk,),
+        grid=(nb,),
         in_specs=[
             pl.BlockSpec((rows, width), lambda j, c: (0, 0)),
-            pl.BlockSpec((None, width, rows), lambda j, c: (jnp.minimum(j, c[0]), 0, 0)),
-            pl.BlockSpec((None, rows, width), lambda j, c: (jnp.minimum(j, c[0]), 0, part)),
+            pl.BlockSpec((group, width, rows), lambda j, c: (jnp.minimum(j, c[0] // group), 0, 0)),
+            pl.BlockSpec((group, rows, width), lambda j, c: (jnp.minimum(j, c[0] // group), 0, part)),
         ],
         out_specs=pl.BlockSpec((rows, width), lambda j, c: (0, 0)),
         scratch_shapes=[
-            pltpu.VMEM((heads, rows, 1), jnp.float32),
-            pltpu.VMEM((heads, rows, 1), jnp.float32),
+            pltpu.VMEM((heads, rows, HDIM), jnp.float32),
+            pltpu.VMEM((heads, rows, HDIM), jnp.float32),
             pltpu.VMEM((heads, rows, HDIM), jnp.float32),
         ],
     )

time: 357 us -> 342 us (0.958)
  Pallas kernels: 66.8 us -> 31.6 us
  waiting for transfers between devices: 162 us -> 181 us
    pallas_call x2, Pallas kernels: 66.8 us -> 31.6 us  [flash_attend(): pl.pallas_call(kernel, grid_spec=grid_spec, out_shape=jax.ShapeDtypeStruc...]
    all_gather x2, waiting for transfers between devices: 53.8 us -> 71.3 us  [local(): lax.all_gather(kt_glob[p * pw:(p + 1) * pw], 'ctx', axis=0, tiled=False)]
  transfers between devices with their start and end apart: 10 -> 10, of which waited for: 9 -> 9; matrix products, arithmetic and copies ran while one was open for 21% -> 22% of each run, Pallas kernels for 9% -> 5%
where the time goes in v2:
time: 342 us; the launch traced here: 338 us
  waiting for transfers between devices  181 us (53%)
  matrix products  81.5 us (24%)
  Pallas kernels  31.6 us (9%)
  local copies, waits for them, and re-layouts  15.5 us (5%)
  between operations  14.1 us (4%)
  starting transfers between devices  9.57 us (3%)
  other arithmetic  4.03 us (1%)
    all_gather x2, waiting for transfers between devices, local(): lax.all_gather(kt_glob[p * pw:(p + 1) * pw], 'ctx', axis=0, tiled=False)  71.3 us
    ppermute x4, waiting for transfers between devices, exclusive_shards(): lax.ppermute(acc, axis, [(i, i + shift) for i in range(length - shift)])  64.8 us
    dot_general x20, matrix products, mm(): return jnp.einsum('...ij,...jk->...ik', a, b, precision=HP)  32.9 us
    pallas_call x2, Pallas kernels, flash_attend(): pl.pallas_call(kernel, grid_spec=grid_spec, out_shape=jax.ShapeDtypeStruc...  31.6 us
    ppermute x1, waiting for transfers between devices, project_out(): got = lax.ppermute(sent, 'hg', SWAP)  23.8 us
    ppermute x1, waiting for transfers between devices, exchange_heads(): lax.ppermute(jnp.where(first, stacked[:, :, 1], stacked[:, :, 0]), 'hg',...  17.2 us
    dot_general x2, matrix products, in_shard(): moved = jnp.einsum('hnid,hned->hnie', inblock, inner_prefix, precision=HP)  14.5 us
    unnamed x23, local copies, waits for them, and re-layouts  7.93 us
  transfers between devices with their start and end apart: 10, of which 9 were waited for; matrix products, arithmetic and copies ran while one was open for 22% of the time, Pallas kernels for 5%

profile of v2, /device:TPU:27, one launch (start us, length us, event | category | flops | bytes accessed | tf_op | source)
XLA Modules:
  0.0 337.5 jit_solution(5216919422141654606)
XLA Ops:
  6.5 1.6 stack.12
  9.1 1.4 stack.13
  10.5 1.4 stack.14
  13.8 1.5 select_bitcast_fusion.1
  15.2 1.3 collective-permute-start
  16.5 17.2 %collective-permute-done = bf16[128,3,1024]{2,0,1:T(8,128)(2,1)S(1)} collective-permute-done((bf16[128,3,1024]{2,0,1:T(8,128)(2,1)S(1)}, bf16[128,3,1024]{2,0,1:T(8,128)(2,1)S(1)}, u32[]{:S(2)}, u32[]{:S(2)}) %collective-permute-start) | collective-permute-done | bytes 786464 | tf_op jit(solution)/shard_map/ppermute | solution.py:154
  35.7 2.2 multiply_reduce_fusion
  38.2 1.8 fusion.14
  40.0 1.2 fusion.55
  41.2 1.2 fusion.56
  42.4 1.2 fusion.57
  43.6 1.2 fusion.58
  44.8 1.2 fusion.59
  46.0 1.2 fusion.23
  47.2 1.2 fusion.21
  48.4 1.2 fusion.19
  49.6 1.4 fusion.17
  55.6 7.1 %convolution_subtract_fusion = f32[8,8,128,128]{3,2,1,0:T(8,128)S(1)} fusion(f32[8,8,32,128]{3,2,1,0:T(8,128)S(1)} %bitcast.111, f32[8,8,32,128]{3,2,1,0:T(8,128)S(1)} %fusion.61, f32[128,128]{1,0:T(8,128)S(1)} %fusion.44), kind=kOutput, calls=%fused_computation.19 | convolution fusion | flops 403701760 | bytes 6356992 | tf_op jit(solution)/shard_map/hnkd,hnke->hnde/dot_general | solution.py:208
  63.6 4.7 %fusion.1 = f32[8,8,128,128]{3,2,1,0:T(8,128)S(1)} fusion(f32[8,1,128,128]{3,2,1,0:T(8,128)S(1)} %broadcast_in_dim.41, f32[8,7,128,128]{3,2,1,0:T(8,128)S(1)} %slice.76, f32[8,7,128,128]{3,2,1,0:T(8,128)S(1)} %fusion.12), kind=kOutput, calls=%fused_computation.7 | convolution fusion | flops 1612709888 | bytes 12058624 | tf_op jit(solution)/shard_map/...ij,...jk->...ik/dot_general | solution.py:17
  68.8 4.7 %fusion.3 = f32[8,8,128,128]{3,2,1,0:T(8,128)S(1)} fusion(f32[8,8,128,128]{3,2,1,0:T(8,128)S(1)} %fusion.1, f32[8,6,128,128]{3,2,1,0:T(8,128)S(1)} %slice.79, f32[8,2,128,128]{3,2,1,0:T(8,128)S(1)} %broadcast_in_dim_broadcast_in_dim.7), kind=kOutput, calls=%fused_computation.9 | convolution fusion | flops 1611661312 | bytes 12582912 | tf_op jit(solution)/shard_map/...ij,...jk->...ik/dot_general | solution.py:17
  73.9 4.9 %fusion.7 = f32[8,8,128,128]{3,2,1,0:T(8,128)S(1)} fusion(f32[8,8,128,128]{3,2,1,0:T(8,128)S(1)} %fusion.3, f32[8,4,128,128]{3,2,1,0:T(8,128)S(1)} %slice.80, f32[8,4,128,128]{3,2,1,0:T(8,128)S(1)} %broadcast_in_dim_broadcast_in_dim.6), kind=kOutput, calls=%fused_computation.13 | convolution fusion | flops 1611661312 | bytes 12582912 | tf_op jit(solution)/shard_map/...ij,...jk->...ik/dot_general | solution.py:17
  78.8 2.0 copy-done.2
  81.5 1.3 collective-permute-start.1
  82.8 3.7 %collective-permute-done.1 = f32[8,128,128]{2,1,0:T(8,128)} collective-permute-done((f32[8,128,128]{2,1,0:T(8,128)S(1)}, f32[8,128,128]{2,1,0:T(8,128)}, u32[]{:S(2)}, u32[]{:S(2)}) %collective-permute-start.1) | collective-permute-done | bytes 524320 | tf_op jit(solution)/shard_map/ppermute | solution.py:50
  87.5 1.3 collective-permute-start.2
  88.8 16.9 %collective-permute-done.2 = f32[8,128,128]{2,1,0:T(8,128)S(1)} collective-permute-done((f32[8,128,128]{2,1,0:T(8,128)S(1)}, f32[8,128,128]{2,1,0:T(8,128)S(1)}, u32[]{:S(2)}, u32[]{:S(2)}) %collective-permute-start.2) | collective-permute-done | bytes 524320 | tf_op jit(solution)/shard_map/ppermute | solution.py:54
  106.3 1.3 collective-permute-start.3
  108.8 12.2 %collective-permute-done.3 = f32[8,128,128]{2,1,0:T(8,128)} collective-permute-done((f32[8,128,128]{2,1,0:T(8,128)S(1)}, f32[8,128,128]{2,1,0:T(8,128)}, u32[]{:S(2)}, u32[]{:S(2)}) %collective-permute-start.3) | collective-permute-done | bytes 524320 | tf_op jit(solution)/shard_map/ppermute | solution.py:54
  121.0 1.7 convolution_select_fusion.5
  122.7 1.3 collective-permute-start.4
  124.9 1.8 fusion.63
  126.7 19.3 %collective-permute-done.4 = f32[8,128,128]{2,1,0:T(8,128)S(1)} collective-permute-done((f32[8,128,128]{2,1,0:T(8,128)S(1)}, f32[8,128,128]{2,1,0:T(8,128)S(1)}, u32[]{:S(2)}, u32[]{:S(2)}) %collective-permute-start.4) | collective-permute-done | bytes 524320 | tf_op jit(solution)/shard_map/ppermute | solution.py:54
  146.7 1.5 collective-permute-start.5
  148.2 1.2 convolution_subtract_fusion.1
  149.5 7.7 %fusion.64 = f32[8,8,32,128]{3,2,1,0:T(8,128)} fusion(f32[8,8,32,128]{3,2,1,0:T(8,128)S(1)} %convolution_subtract_fusion.1, f32[8,8,128,128]{3,2,1,0:T(8,128)S(1)} %copy-done.3), kind=kOutput, calls=%fused_computation.102 | convolution fusion | flops 402653184 | bytes 6291456 | tf_op jit(solution)/shard_map/hnid,hned->hnie/dot_general | solution.py:220
  157.2 16.4 %collective-permute-done.5 = f32[8,128,128]{2,1,0:T(8,128)S(1)} collective-permute-done((f32[8,128,128]{2,1,0:T(8,128)S(1)}, f32[8,128,128]{2,1,0:T(8,128)S(1)}, u32[]{:S(2)}, u32[]{:S(2)}) %collective-permute-start.5) | collective-permute-done | bytes 524320 | tf_op jit(solution)/shard_map/ppermute | solution.py:54
  174.3 2.3 convolution_convert_fusion.1
  179.2 1.8 fusion.60
  181.0 1.2 convolution_subtract_fusion.2
  182.3 6.8 %fusion.62 = f32[8,8,32,128]{3,2,1,0:T(8,128)S(1)} fusion(f32[8,8,32,128]{3,2,1,0:T(8,128)S(1)} %convolution_subtract_fusion.2, f32[8,8,128,128]{3,2,1,0:T(8,128)S(1)} %copy-done.4), kind=kOutput, calls=%fused_computation.100 | convolution fusion | flops 402653184 | bytes 6291456 | tf_op jit(solution)/shard_map/hnid,hned->hnie/dot_general | solution.py:220
  191.8 36.0 %all-gather.7.cloned.1.call-done.k_ref = bf16[16,512,256]{2,1,0:T(8,128)(2,1)} async-done(((bf16[1,512,256]{2,1,0:T(8,128)(2,1)}), bf16[16,512,256]{2,1,0:T(8,128)(2,1)}) %all-gather.7.cloned.1.call-update) | async-done | bytes 4194320 | tf_op jit(solution)/shard_map/all_gather | solution.py:229
  227.9 16.0 %shard_map.65 = bf16[256,512]{1,0:T(8,128)(2,1)} custom-call(s32[1]{0:T(128)} %bitcast.c_ref, bf16[256,512]{1,0:T(8,128)(2,1)} %copy.28.q_ref, bf16[16,512,256]{2,1,0:T(8,128)(2,1)} %all-gather.7.cloned.1.call-done.k_ref, bf16[16,256,1024]{2,1,0:T(8,128)(2,1)} %bitcast.116), custom_call_target="tpu_custom_call" | custom-call | tf_op jit(solution)/shard_map/pallas_call | solution.py:138
  243.8 35.3 %all-gather.5.cloned.1.call-done.k_ref = bf16[16,512,256]{2,1,0:T(8,128)(2,1)} async-done(((bf16[1,512,256]{2,1,0:T(8,128)(2,1)}), bf16[16,512,256]{2,1,0:T(8,128)(2,1)}) %all-gather.5.cloned.1.call-update) | async-done | bytes 4194320 | tf_op jit(solution)/shard_map/all_gather | solution.py:229
  279.1 15.6 %shard_map.64 = bf16[256,512]{1,0:T(8,128)(2,1)} custom-call(s32[1]{0:T(128)} %bitcast.c_ref, bf16[256,512]{1,0:T(8,128)(2,1)} %copy.27.q_ref, bf16[16,512,256]{2,1,0:T(8,128)(2,1)} %all-gather.5.cloned.1.call-done.k_ref, bf16[16,256,1024]{2,1,0:T(8,128)(2,1)} %bitcast.117), custom_call_target="tpu_custom_call" | custom-call | tf_op jit(solution)/shard_map/pallas_call | solution.py:138
  294.7 4.8 %convolution_convert_fusion = bf16[128,4096]{1,0:T(8,128)(2,1)S(1)} fusion(bf16[1024,4096]{1,0:T(8,128)(2,1)} %param.11, pred[]{:T(512)S(6)} %eq.55, bf16[256,512]{1,0:T(8,128)(2,1)S(1)} %copy-done.5, bf16[256,512]{1,0:T(8,128)(2,1)} %shard_map.64), kind=kOutput, calls=%fused_computation.5 | convolution fusion | flops 1075445760 | bytes 9961473 | tf_op jit(solution)/shard_map/dot_general | solution.py:172
  299.6 1.3 collective-permute-start.6
  300.8 23.8 %collective-permute-done.6 = bf16[128,4096]{1,0:T(8,128)(2,1)S(1)} collective-permute-done((bf16[128,4096]{1,0:T(8,128)(2,1)S(1)}, bf16[128,4096]{1,0:T(8,128)(2,1)S(1)}, u32[]{:S(2)}, u32[]{:S(2)}) %collective-permute-start.6) | collective-permute-done | bytes 1048608 | tf_op jit(solution)/shard_map/ppermute | solution.py:173
  324.7 5.8 %add_convert_fusion = bf16[128,4096]{1,0:T(8,128)(2,1)} fusion(bf16[128,4096]{1,0:T(8,128)(2,1)S(1)} %collective-permute-done.6, bf16[1024,4096]{1,0:T(8,128)(2,1)} %param.11, pred[]{:T(512)S(6)} %eq.55, bf16[256,512]{1,0:T(8,128)(2,1)S(1)} %copy-done.5, bf16[256,512]{1,0:T(8,128)(2,1)S(1)} %copy-done.6), kind=kOutput, calls=%fused_computation.22 | convolution fusion | flops 1076494336 | bytes 11010049 | tf_op jit(solution)/shard_map/dot_general | solution.py:174
  (57 shorter events, 22.7 us)
Async XLA Ops:
  6.5 29.2 %copy-start = (bf16[1024,1024]{1,0:T(8,128)(2,1)S(1)}, bf16[1024,1024]{1,0:T(8,128)(2,1)}, u32[]{:S(2)}) copy-start(bf16[1024,1024]{1,0:T(8,128)(2,1)} %param.10) | copy-start | bytes 6291460
  6.5 167.8 %all-gather.9.cloned.1.call-start = ((), (), s32[]{:S(2)}) async-start(), calls=%async_computation.2 | async-start | bytes 8912896 | tf_op jit(solution)/shard_map/all_gather | solution.py:190
  15.2 20.5 %copy-start.7 = (s32[256,8]{0,1:T(8,128)S(1)}, s32[256,8]{0,1:T(8,128)}, u32[]{:S(2)}) copy-start(s32[256,8]{0,1:T(8,128)} %param.9) | copy-start | bytes 24580
  15.2 18.5 %collective-permute-start = (bf16[128,3,1024]{2,0,1:T(8,128)(2,1)S(1)}, bf16[128,3,1024]{2,0,1:T(8,128)(2,1)S(1)}, u32[]{:S(2)}, u32[]{:S(2)}) collective-permute-start(bf16[128,3,1024]{2,0,1:T(8,128)(2,1)S(1)} %get-tuple-element.17), channel_id=1, source_target_pairs={{0,1},{1,0},{2,3},{3,2},{4,5},{5,4},{6,7},{7,6},{8,9},{9,8},{10,11... | collective-permute-start | bytes 2359304 | tf_op jit(solution)/shard_map/ppermute | solution.py:154
  35.6 192.3 %all-gather.7.cloned.1.call-start = ((), (), s32[]{:S(2)}) async-start(), calls=%async_computation.1 | async-start | bytes 4456448 | tf_op jit(solution)/shard_map/all_gather | solution.py:229
  78.8 2.0 copy-start.2
  81.5 5.0 %collective-permute-start.1 = (f32[8,128,128]{2,1,0:T(8,128)S(1)}, f32[8,128,128]{2,1,0:T(8,128)}, u32[]{:S(2)}, u32[]{:S(2)}) collective-permute-start(f32[8,128,128]{2,1,0:T(8,128)S(1)} %fusion.26), channel_id=1, source_target_pairs={{0,2},{2,4},{4,6},{6,8},{8,10},{10,12},{12,14},{14,16},{16,18},{18... | collective-permute-start | bytes 1572872 | tf_op jit(solution)/shard_map/ppermute | solution.py:50
  87.5 18.2 %collective-permute-start.2 = (f32[8,128,128]{2,1,0:T(8,128)S(1)}, f32[8,128,128]{2,1,0:T(8,128)S(1)}, u32[]{:S(2)}, u32[]{:S(2)}) collective-permute-start(f32[8,128,128]{2,1,0:T(8,128)S(1)} %broadcast_select_fusion), channel_id=1, source_target_pairs={{0,2},{2,4},{4,6},{6,8},{8,10},{10,12},{12,14},{14,16},{16,18},{18... | collective-permute-start | bytes 1572872 | tf_op jit(solution)/shard_map/ppermute | solution.py:54
  106.3 14.6 %collective-permute-start.3 = (f32[8,128,128]{2,1,0:T(8,128)S(1)}, f32[8,128,128]{2,1,0:T(8,128)}, u32[]{:S(2)}, u32[]{:S(2)}) collective-permute-start(f32[8,128,128]{2,1,0:T(8,128)S(1)} %convolution_select_fusion.6), channel_id=1, source_target_pairs={{0,4},{2,6},{4,8},{6,10},{8,12},{10,14},{12,16},{14,18},{16,20},{1... | collective-permute-start | bytes 1572872 | tf_op jit(solution)/shard_map/ppermute | solution.py:54
  122.7 23.4 %collective-permute-start.4 = (f32[8,128,128]{2,1,0:T(8,128)S(1)}, f32[8,128,128]{2,1,0:T(8,128)S(1)}, u32[]{:S(2)}, u32[]{:S(2)}) collective-permute-start(f32[8,128,128]{2,1,0:T(8,128)S(1)} %convolution_select_fusion.5), channel_id=1, source_target_pairs={{0,8},{2,10},{4,12},{6,14},{8,16},{10,18},{12,20},{14,22},{16,24},... | collective-permute-start | bytes 1572872 | tf_op jit(solution)/shard_map/ppermute | solution.py:54
  124.9 24.5 %copy-start.3 = (f32[8,8,128,128]{3,2,1,0:T(8,128)S(1)}, f32[8,8,128,128]{3,2,1,0:T(8,128)}, u32[]{:S(2)}) copy-start(f32[8,8,128,128]{3,2,1,0:T(8,128)} %copy-done.2) | copy-start | bytes 12582916
  146.7 26.9 %collective-permute-start.5 = (f32[8,128,128]{2,1,0:T(8,128)S(1)}, f32[8,128,128]{2,1,0:T(8,128)S(1)}, u32[]{:S(2)}, u32[]{:S(2)}) collective-permute-start(f32[8,128,128]{2,1,0:T(8,128)S(1)} %convolution_select_fusion.4), channel_id=1, source_target_pairs={{0,16},{2,18},{4,20},{6,22},{8,24},{10,26},{12,28},{14,30},{1,17},... | collective-permute-start | bytes 1572872 | tf_op jit(solution)/shard_map/ppermute | solution.py:54
  177.4 101.7 %all-gather.5.cloned.1.call-start = ((), (), s32[]{:S(2)}) async-start(), calls=%async_computation | async-start | bytes 4456448 | tf_op jit(solution)/shard_map/all_gather | solution.py:229
  179.2 3.0 copy-start.4
  243.8 50.9 %copy-start.5 = (bf16[256,512]{1,0:T(8,128)(2,1)S(1)}, bf16[256,512]{1,0:T(8,128)(2,1)}, u32[]{:S(2)}) copy-start(bf16[256,512]{1,0:T(8,128)(2,1)} %shard_map.65) | copy-start | bytes 786436
  294.7 30.0 %copy-start.6 = (bf16[256,512]{1,0:T(8,128)(2,1)S(1)}, bf16[256,512]{1,0:T(8,128)(2,1)}, u32[]{:S(2)}) copy-start(bf16[256,512]{1,0:T(8,128)(2,1)} %shard_map.64) | copy-start | bytes 786436
  299.6 25.1 %collective-permute-start.6 = (bf16[128,4096]{1,0:T(8,128)(2,1)S(1)}, bf16[128,4096]{1,0:T(8,128)(2,1)S(1)}, u32[]{:S(2)}, u32[]{:S(2)}) collective-permute-start(bf16[128,4096]{1,0:T(8,128)(2,1)S(1)} %convolution_convert_fusion), channel_id=1, source_target_pairs={{0,1},{1,0},{2,3},{3,2},{4,5},{5,4},{6,7},{7,6},{8,9},{9,8},{10,11... | collective-permute-start | bytes 3145736 | tf_op jit(solution)/shard_map/ppermute | solution.py:173
  324.7 5.8 %copy-start.1 = (bf16[1024,1024]{1,0:T(8,128)(2,1)S(1)}, bf16[1024,1024]{1,0:T(8,128)(2,1)}, u32[]{:S(2)}) copy-start(bf16[1024,1024]{1,0:T(8,128)(2,1)} %param.10) | copy-start | bytes 6291460
Sparse Core Ops, SparseCore 0:
  35.7 79.5 all-gather.8
  177.6 50.2 all-gather.6
  230.0 49.0 all-gather.4

commit v3 on v2

--- a/solution.py
+++ b/solution.py
@@ -157,22 +157,29 @@
     )
 
 
-def project_out(attn, out_weight, groups):
+def project_out(parts, out_weight, w_other, groups):
     if groups != 2:
         return lax.psum_scatter(
-            jnp.dot(attn, out_weight, preferred_element_type=jnp.float32).astype(jnp.bfloat16),
+            jnp.dot(
+                jnp.concatenate(parts, axis=1), out_weight, preferred_element_type=jnp.float32
+            ).astype(jnp.bfloat16),
             "hg",
             scatter_dimension=0,
             tiled=True,
         )
-    half = attn.shape[0] // 2
+    half = parts[0].shape[0] // 2
     first = lax.axis_index("hg") == 0
-    theirs = jnp.where(first, attn[half:], attn[:half])
-    mine = jnp.where(first, attn[:half], attn[half:])
-    sent = jnp.dot(theirs, out_weight, preferred_element_type=jnp.float32).astype(jnp.bfloat16)
-    got = lax.ppermute(sent, "hg", SWAP)
-    kept = jnp.dot(mine, out_weight, preferred_element_type=jnp.float32)
-    return (kept + got.astype(jnp.float32)).astype(jnp.bfloat16)
+    got = [
+        lax.ppermute(jnp.where(first, a[half:], a[:half]), "hg", SWAP) for a in parts
+    ]
+    mine = jnp.concatenate([jnp.where(first, a[:half], a[half:]) for a in parts], axis=1)
+    total = jnp.dot(mine, out_weight, preferred_element_type=jnp.float32)
+    pw = parts[0].shape[1]
+    for p, a in enumerate(got):
+        total = total + jnp.dot(
+            a, w_other[p * pw : (p + 1) * pw], preferred_element_type=jnp.float32
+        )
+    return total.astype(jnp.bfloat16)
 
 
 def local(queries, keys, values, reflect_ids, reflect_bank, out_weight):
@@ -209,7 +216,10 @@
     lower_mask = jnp.tril(jnp.ones((BLK, BLK), dtype=jnp.bool_))
 
     inner_prefix, shard_prod = exclusive_blocks(block_mats)
-    earlier_prod, v_all = lax.optimization_barrier((exclusive_shards(shard_prod, "ctx"), v_all))
+    w_other = lax.ppermute(out_weight, "hg", SWAP) if groups == 2 else None
+    earlier_prod, v_all, w_other = lax.optimization_barrier(
+        (exclusive_shards(shard_prod, "ctx"), v_all, w_other)
+    )
 
     def in_shard(matrix):
         split = matrix.astype(jnp.float32).reshape(nblocks, BLK, heads, HDIM).transpose(2, 0, 1, 3)
@@ -236,14 +246,11 @@
         .astype(jnp.bfloat16)
     )
     shard = lax.axis_index("ctx")
-    attn = jnp.concatenate(
-        [
-            flash_attend(q_glob[:, p * pw : (p + 1) * pw], kt_parts[p], v_all, p, shard, heads // parts)
-            for p in range(parts)
-        ],
-        axis=1,
-    )
-    return project_out(attn, out_weight, groups)
+    attn = [
+        flash_attend(q_glob[:, p * pw : (p + 1) * pw], kt_parts[p], v_all, p, shard, heads // parts)
+        for p in range(parts)
+    ]
+    return project_out(attn, out_weight, w_other, groups)
 
 
 def solution(mesh):

time: 342 us -> 364 us (1.064)
  waiting for transfers between devices: 181 us -> 199 us
    ppermute x1 -> x3, waiting for transfers between devices: 23.8 us -> 42.4 us  [the longest x1 42.4 us: local(): w_other = lax.ppermute(out_weight, 'hg', SWAP) if groups == 2 else None]
    dot_general x2 -> x3, matrix products: 10.7 us -> 11.9 us  [the longest x2 7.14 us: project_out(): jnp.dot(a, w_other[p * pw:(p + 1) * pw], preferred_element_type=jnp.float32)]
    unnamed x23 -> x19, local copies, waits for them, and re-layouts: 7.93 us -> 7.86 us
  transfers between devices with their start and end apart: 10 -> 12, of which waited for: 9 -> 9; matrix products, arithmetic and copies ran while one was open for 22% -> 23% of each run, Pallas kernels for 5% -> 4%
where the time goes in v3:
time: 364 us; the launch traced here: 360 us
  waiting for transfers between devices  199 us (55%)
  matrix products  82.7 us (23%)
  Pallas kernels  31.5 us (9%)
  local copies, waits for them, and re-layouts  15.5 us (4%)
  between operations  14.1 us (4%)
  starting transfers between devices  11.2 us (3%)
  other arithmetic  6.01 us (2%)
    all_gather x2, waiting for transfers between devices, local(): lax.all_gather(kt_glob[p * pw:(p + 1) * pw], 'ctx', axis=0, tiled=False)  71.6 us
    ppermute x4, waiting for transfers between devices, exclusive_shards(): lax.ppermute(acc, axis, [(i, i + shift) for i in range(length - shift)])  63.1 us
    ppermute x1, waiting for transfers between devices, local(): w_other = lax.ppermute(out_weight, 'hg', SWAP) if groups == 2 else None  42.4 us
    dot_general x20, matrix products, mm(): return jnp.einsum('...ij,...jk->...ik', a, b, precision=HP)  32.9 us
    pallas_call x2, Pallas kernels, flash_attend(): pl.pallas_call(kernel, grid_spec=grid_spec, out_shape=jax.ShapeDtypeStruc...  31.5 us
    ppermute x1, waiting for transfers between devices, exchange_heads(): lax.ppermute(jnp.where(first, stacked[:, :, 1], stacked[:, :, 0]), 'hg',...  17.2 us
    dot_general x2, matrix products, in_shard(): moved = jnp.einsum('hnid,hned->hnie', inblock, inner_prefix, precision=HP)  14.5 us
    unnamed x19, local copies, waits for them, and re-layouts  7.86 us
  transfers between devices with their start and end apart: 12, of which 9 were waited for; matrix products, arithmetic and copies ran while one was open for 23% of the time, Pallas kernels for 4%

profile of v3, /device:TPU:27, one launch (start us, length us, event | category | flops | bytes accessed | tf_op | source)
XLA Modules:
  0.0 359.6 jit_solution(1805144285413405217)
XLA Ops:
  6.5 1.6 stack.12
  9.1 1.4 stack.13
  10.5 1.4 stack.14
  13.8 1.5 select_bitcast_fusion.1
  15.3 1.3 collective-permute-start
  16.6 17.2 %collective-permute-done = bf16[128,3,1024]{2,0,1:T(8,128)(2,1)S(1)} collective-permute-done((bf16[128,3,1024]{2,0,1:T(8,128)(2,1)S(1)}, bf16[128,3,1024]{2,0,1:T(8,128)(2,1)S(1)}, u32[]{:S(2)}, u32[]{:S(2)}) %collective-permute-start) | collective-permute-done | bytes 786464 | tf_op jit(solution)/shard_map/ppermute | solution.py:154
  35.6 1.3 collective-permute-start.6
  37.0 2.2 multiply_reduce_fusion
  39.5 1.7 fusion.17
  42.4 1.2 fusion.52
  43.6 1.2 fusion.53
  44.8 1.2 fusion.54
  46.0 1.2 fusion.26
  47.2 1.2 fusion.55
  48.4 1.2 fusion.24
  50.8 1.4 fusion.20
  56.9 7.1 %convolution_subtract_fusion = f32[8,8,128,128]{3,2,1,0:T(8,128)S(1)} fusion(f32[8,8,32,128]{3,2,1,0:T(8,128)S(1)} %bitcast.112, f32[8,8,32,128]{3,2,1,0:T(8,128)S(1)} %fusion.57, f32[128,128]{1,0:T(8,128)S(1)} %fusion.43), kind=kOutput, calls=%fused_computation.23 | convolution fusion | flops 403701760 | bytes 6356992 | tf_op jit(solution)/shard_map/hnkd,hnke->hnde/dot_general | solution.py:215
  64.9 4.7 %fusion.2 = f32[8,8,128,128]{3,2,1,0:T(8,128)S(1)} fusion(f32[8,1,128,128]{3,2,1,0:T(8,128)S(1)} %broadcast_in_dim.41, f32[8,7,128,128]{3,2,1,0:T(8,128)S(1)} %slice.94, f32[8,7,128,128]{3,2,1,0:T(8,128)S(1)} %fusion.15), kind=kOutput, calls=%fused_computation.9 | convolution fusion | flops 1612709888 | bytes 12058624 | tf_op jit(solution)/shard_map/...ij,...jk->...ik/dot_general | solution.py:17
  70.0 4.7 %fusion.4 = f32[8,8,128,128]{3,2,1,0:T(8,128)S(1)} fusion(f32[8,8,128,128]{3,2,1,0:T(8,128)S(1)} %fusion.2, f32[8,6,128,128]{3,2,1,0:T(8,128)S(1)} %slice.97, f32[8,2,128,128]{3,2,1,0:T(8,128)S(1)} %broadcast_in_dim_broadcast_in_dim.7), kind=kOutput, calls=%fused_computation.11 | convolution fusion | flops 1611661312 | bytes 12582912 | tf_op jit(solution)/shard_map/...ij,...jk->...ik/dot_general | solution.py:17
  75.2 4.9 %fusion.8 = f32[8,8,128,128]{3,2,1,0:T(8,128)S(1)} fusion(f32[8,8,128,128]{3,2,1,0:T(8,128)S(1)} %fusion.4, f32[8,4,128,128]{3,2,1,0:T(8,128)S(1)} %slice.98, f32[8,4,128,128]{3,2,1,0:T(8,128)S(1)} %broadcast_in_dim_broadcast_in_dim.6), kind=kOutput, calls=%fused_computation.15 | convolution fusion | flops 1611661312 | bytes 12582912 | tf_op jit(solution)/shard_map/...ij,...jk->...ik/dot_general | solution.py:17
  80.1 1.9 copy-done.2
  82.6 1.3 collective-permute-start.1
  84.0 4.0 %collective-permute-done.1 = f32[8,128,128]{2,1,0:T(8,128)} collective-permute-done((f32[8,128,128]{2,1,0:T(8,128)S(1)}, f32[8,128,128]{2,1,0:T(8,128)}, u32[]{:S(2)}, u32[]{:S(2)}) %collective-permute-start.1) | collective-permute-done | bytes 524320 | tf_op jit(solution)/shard_map/ppermute | solution.py:50
  89.0 1.3 collective-permute-start.2
  90.3 15.4 %collective-permute-done.2 = f32[8,128,128]{2,1,0:T(8,128)S(1)} collective-permute-done((f32[8,128,128]{2,1,0:T(8,128)S(1)}, f32[8,128,128]{2,1,0:T(8,128)S(1)}, u32[]{:S(2)}, u32[]{:S(2)}) %collective-permute-start.2) | collective-permute-done | bytes 524320 | tf_op jit(solution)/shard_map/ppermute | solution.py:54
  106.3 1.3 collective-permute-start.3
  108.8 12.5 %collective-permute-done.3 = f32[8,128,128]{2,1,0:T(8,128)} collective-permute-done((f32[8,128,128]{2,1,0:T(8,128)S(1)}, f32[8,128,128]{2,1,0:T(8,128)}, u32[]{:S(2)}, u32[]{:S(2)}) %collective-permute-start.3) | collective-permute-done | bytes 524320 | tf_op jit(solution)/shard_map/ppermute | solution.py:54
  121.2 1.7 convolution_select_fusion.5
  122.9 1.3 collective-permute-start.4
  125.2 1.8 fusion.59
  127.0 18.8 %collective-permute-done.4 = f32[8,128,128]{2,1,0:T(8,128)S(1)} collective-permute-done((f32[8,128,128]{2,1,0:T(8,128)S(1)}, f32[8,128,128]{2,1,0:T(8,128)S(1)}, u32[]{:S(2)}, u32[]{:S(2)}) %collective-permute-start.4) | collective-permute-done | bytes 524320 | tf_op jit(solution)/shard_map/ppermute | solution.py:54
  146.4 1.5 collective-permute-start.5
  148.0 1.2 convolution_subtract_fusion.1
  149.2 7.7 %fusion.60 = f32[8,8,32,128]{3,2,1,0:T(8,128)} fusion(f32[8,8,32,128]{3,2,1,0:T(8,128)S(1)} %convolution_subtract_fusion.1, f32[8,8,128,128]{3,2,1,0:T(8,128)S(1)} %copy-done.3), kind=kOutput, calls=%fused_computation.103 | convolution fusion | flops 402653184 | bytes 6291456 | tf_op jit(solution)/shard_map/hnid,hned->hnie/dot_general | solution.py:230
  156.9 16.4 %collective-permute-done.5 = f32[8,128,128]{2,1,0:T(8,128)S(1)} collective-permute-done((f32[8,128,128]{2,1,0:T(8,128)S(1)}, f32[8,128,128]{2,1,0:T(8,128)S(1)}, u32[]{:S(2)}, u32[]{:S(2)}) %collective-permute-start.5) | collective-permute-done | bytes 524320 | tf_op jit(solution)/shard_map/ppermute | solution.py:54
  174.0 42.4 %collective-permute-done.6 = bf16[1024,4096]{1,0:T(8,128)(2,1)} collective-permute-done((bf16[1024,4096]{1,0:T(8,128)(2,1)}, bf16[1024,4096]{1,0:T(8,128)(2,1)}, u32[]{:S(2)}, u32[]{:S(2)}) %collective-permute-start.6) | collective-permute-done | bytes 8388640 | tf_op jit(solution)/shard_map/ppermute | solution.py:219
  216.4 2.3 convolution_convert_fusion
  221.4 1.8 fusion.56
  223.2 1.2 convolution_subtract_fusion.2
  224.4 6.8 %fusion.58 = f32[8,8,32,128]{3,2,1,0:T(8,128)S(1)} fusion(f32[8,8,32,128]{3,2,1,0:T(8,128)S(1)} %convolution_subtract_fusion.2, f32[8,8,128,128]{3,2,1,0:T(8,128)S(1)} %copy-done.4), kind=kOutput, calls=%fused_computation.101 | convolution fusion | flops 402653184 | bytes 6291456 | tf_op jit(solution)/shard_map/hnid,hned->hnie/dot_general | solution.py:230
  234.0 37.3 %all-gather.7.cloned.1.call-done.k_ref = bf16[16,512,256]{2,1,0:T(8,128)(2,1)} async-done(((bf16[1,512,256]{2,1,0:T(8,128)(2,1)}), bf16[16,512,256]{2,1,0:T(8,128)(2,1)}) %all-gather.7.cloned.1.call-update) | async-done | bytes 4194320 | tf_op jit(solution)/shard_map/all_gather | solution.py:239
  271.2 15.9 %shard_map.65 = bf16[256,512]{1,0:T(8,128)(2,1)} custom-call(s32[1]{0:T(128)} %bitcast.c_ref, bf16[256,512]{1,0:T(8,128)(2,1)} %copy.28.q_ref, bf16[16,512,256]{2,1,0:T(8,128)(2,1)} %all-gather.7.cloned.1.call-done.k_ref, bf16[16,256,1024]{2,1,0:T(8,128)(2,1)} %bitcast.117), custom_call_target="tpu_custom_call" | custom-call | tf_op jit(solution)/shard_map/pallas_call | solution.py:138
  288.1 34.3 %all-gather.5.cloned.1.call-done.k_ref = bf16[16,512,256]{2,1,0:T(8,128)(2,1)} async-done(((bf16[1,512,256]{2,1,0:T(8,128)(2,1)}), bf16[16,512,256]{2,1,0:T(8,128)(2,1)}) %all-gather.5.cloned.1.call-update) | async-done | bytes 4194320 | tf_op jit(solution)/shard_map/all_gather | solution.py:239
  322.5 15.6 %shard_map.64 = bf16[256,512]{1,0:T(8,128)(2,1)} custom-call(s32[1]{0:T(128)} %bitcast.c_ref, bf16[256,512]{1,0:T(8,128)(2,1)} %copy.27.q_ref, bf16[16,512,256]{2,1,0:T(8,128)(2,1)} %all-gather.5.cloned.1.call-done.k_ref, bf16[16,256,1024]{2,1,0:T(8,128)(2,1)} %bitcast.118), custom_call_target="tpu_custom_call" | custom-call | tf_op jit(solution)/shard_map/pallas_call | solution.py:138
  339.1 1.3 collective-permute-start.7
  340.6 4.7 %fusion.39 = f32[128,4096]{1,0:T(8,128)S(1)} fusion(bf16[1024,4096]{1,0:T(8,128)(2,1)} %param.11, bf16[128,512]{1,0:T(8,128)(2,1)S(1)} %get-tuple-element.25, bf16[128,512]{1,0:T(8,128)(2,1)S(1)} %get-tuple-element.27), kind=kOutput, calls=%fused_computation.73 | convolution fusion | flops 1074266112 | bytes 10747904 | tf_op jit(solution)/shard_map/dot_general | solution.py:176
  345.4 3.2 convolution_add_fusion.1
  348.5 4.0 %fusion.1 = bf16[128,4096]{1,0:T(8,128)(2,1)} fusion(f32[128,4096]{1,0:T(8,128)S(1)} %convolution_add_fusion.1, bf16[128,512]{1,0:T(8,128)(2,1)S(1)} %collective-permute-done.8, bf16[1024,4096]{1,0:T(8,128)(2,1)} %collective-permute-done.6), kind=kOutput, calls=%fused_computation.7 | convolution fusion | flops 537919488 | bytes 7471104 | tf_op jit(solution)/shard_map/dot_general | solution.py:179
  (60 shorter events, 27.3 us)
Async XLA Ops:
  6.5 30.4 %copy-start = (bf16[1024,1024]{1,0:T(8,128)(2,1)S(1)}, bf16[1024,1024]{1,0:T(8,128)(2,1)}, u32[]{:S(2)}) copy-start(bf16[1024,1024]{1,0:T(8,128)(2,1)} %param.10) | copy-start | bytes 6291460
  6.5 209.9 %all-gather.9.cloned.1.call-start = ((), (), s32[]{:S(2)}) async-start(), calls=%async_computation.2 | async-start | bytes 8912896 | tf_op jit(solution)/shard_map/all_gather | solution.py:197
  15.2 21.7 %copy-start.5 = (s32[256,8]{0,1:T(8,128)S(1)}, s32[256,8]{0,1:T(8,128)}, u32[]{:S(2)}) copy-start(s32[256,8]{0,1:T(8,128)} %param.9) | copy-start | bytes 24580
  15.3 18.5 %collective-permute-start = (bf16[128,3,1024]{2,0,1:T(8,128)(2,1)S(1)}, bf16[128,3,1024]{2,0,1:T(8,128)(2,1)S(1)}, u32[]{:S(2)}, u32[]{:S(2)}) collective-permute-start(bf16[128,3,1024]{2,0,1:T(8,128)(2,1)S(1)} %get-tuple-element.19), channel_id=1, source_target_pairs={{0,1},{1,0},{2,3},{3,2},{4,5},{5,4},{6,7},{7,6},{8,9},{9,8},{10,11... | collective-permute-start | bytes 2359304 | tf_op jit(solution)/shard_map/ppermute | solution.py:154
  35.6 235.6 %all-gather.7.cloned.1.call-start = ((), (), s32[]{:S(2)}) async-start(), calls=%async_computation.1 | async-start | bytes 4456448 | tf_op jit(solution)/shard_map/all_gather | solution.py:239
  35.6 180.8 %collective-permute-start.6 = (bf16[1024,4096]{1,0:T(8,128)(2,1)}, bf16[1024,4096]{1,0:T(8,128)(2,1)}, u32[]{:S(2)}, u32[]{:S(2)}) collective-permute-start(bf16[1024,4096]{1,0:T(8,128)(2,1)} %param.11), channel_id=1, source_target_pairs={{0,1},{1,0},{2,3},{3,2},{4,5},{5,4},{6,7},{7,6},{8,9},{9,8},{10,11... | collective-permute-start | bytes 25165832 | tf_op jit(solution)/shard_map/ppermute | solution.py:219
  80.1 1.9 copy-start.2
  82.6 5.3 %collective-permute-start.1 = (f32[8,128,128]{2,1,0:T(8,128)S(1)}, f32[8,128,128]{2,1,0:T(8,128)}, u32[]{:S(2)}, u32[]{:S(2)}) collective-permute-start(f32[8,128,128]{2,1,0:T(8,128)S(1)} %fusion.29), channel_id=1, source_target_pairs={{0,2},{2,4},{4,6},{6,8},{8,10},{10,12},{12,14},{14,16},{16,18},{18... | collective-permute-start | bytes 1572872 | tf_op jit(solution)/shard_map/ppermute | solution.py:50
  89.0 16.7 %collective-permute-start.2 = (f32[8,128,128]{2,1,0:T(8,128)S(1)}, f32[8,128,128]{2,1,0:T(8,128)S(1)}, u32[]{:S(2)}, u32[]{:S(2)}) collective-permute-start(f32[8,128,128]{2,1,0:T(8,128)S(1)} %broadcast_select_fusion), channel_id=1, source_target_pairs={{0,2},{2,4},{4,6},{6,8},{8,10},{10,12},{12,14},{14,16},{16,18},{18... | collective-permute-start | bytes 1572872 | tf_op jit(solution)/shard_map/ppermute | solution.py:54
  106.3 14.9 %collective-permute-start.3 = (f32[8,128,128]{2,1,0:T(8,128)S(1)}, f32[8,128,128]{2,1,0:T(8,128)}, u32[]{:S(2)}, u32[]{:S(2)}) collective-permute-start(f32[8,128,128]{2,1,0:T(8,128)S(1)} %convolution_select_fusion.6), channel_id=1, source_target_pairs={{0,4},{2,6},{4,8},{6,10},{8,12},{10,14},{12,16},{14,18},{16,20},{1... | collective-permute-start | bytes 1572872 | tf_op jit(solution)/shard_map/ppermute | solution.py:54
  122.9 22.8 %collective-permute-start.4 = (f32[8,128,128]{2,1,0:T(8,128)S(1)}, f32[8,128,128]{2,1,0:T(8,128)S(1)}, u32[]{:S(2)}, u32[]{:S(2)}) collective-permute-start(f32[8,128,128]{2,1,0:T(8,128)S(1)} %convolution_select_fusion.5), channel_id=1, source_target_pairs={{0,8},{2,10},{4,12},{6,14},{8,16},{10,18},{12,20},{14,22},{16,24},... | collective-permute-start | bytes 1572872 | tf_op jit(solution)/shard_map/ppermute | solution.py:54
  125.2 24.0 %copy-start.3 = (f32[8,8,128,128]{3,2,1,0:T(8,128)S(1)}, f32[8,8,128,128]{3,2,1,0:T(8,128)}, u32[]{:S(2)}) copy-start(f32[8,8,128,128]{3,2,1,0:T(8,128)} %copy-done.2) | copy-start | bytes 12582916
  146.4 26.9 %collective-permute-start.5 = (f32[8,128,128]{2,1,0:T(8,128)S(1)}, f32[8,128,128]{2,1,0:T(8,128)S(1)}, u32[]{:S(2)}, u32[]{:S(2)}) collective-permute-start(f32[8,128,128]{2,1,0:T(8,128)S(1)} %convolution_select_fusion.4), channel_id=1, source_target_pairs={{0,16},{2,18},{4,20},{6,22},{8,24},{10,26},{12,28},{14,30},{1,17},... | collective-permute-start | bytes 1572872 | tf_op jit(solution)/shard_map/ppermute | solution.py:54
  219.6 102.9 %all-gather.5.cloned.1.call-start = ((), (), s32[]{:S(2)}) async-start(), calls=%async_computation | async-start | bytes 4456448 | tf_op jit(solution)/shard_map/all_gather | solution.py:239
  220.4 4.0 %copy-start.4 = (f32[8,8,128,128]{3,2,1,0:T(8,128)S(1)}, f32[8,8,128,128]{3,2,1,0:T(8,128)}, u32[]{:S(2)}) copy-start(f32[8,8,128,128]{3,2,1,0:T(8,128)} %copy-done.2) | copy-start | bytes 12582916
  339.1 6.3 %collective-permute-start.7 = (bf16[128,512]{1,0:T(8,128)(2,1)S(1)}, bf16[128,512]{1,0:T(8,128)(2,1)S(1)}, u32[]{:S(2)}, u32[]{:S(2)}) collective-permute-start(bf16[128,512]{1,0:T(8,128)(2,1)S(1)} %get-tuple-element.26), channel_id=1, source_target_pairs={{0,1},{1,0},{2,3},{3,2},{4,5},{5,4},{6,7},{7,6},{8,9},{9,8},{10,11... | collective-permute-start | bytes 393224 | tf_op jit(solution)/shard_map/ppermute | solution.py:173
  340.3 8.2 %collective-permute-start.8 = (bf16[128,512]{1,0:T(8,128)(2,1)S(1)}, bf16[128,512]{1,0:T(8,128)(2,1)S(1)}, u32[]{:S(2)}, u32[]{:S(2)}) collective-permute-start(bf16[128,512]{1,0:T(8,128)(2,1)S(1)} %get-tuple-element.24), channel_id=1, source_target_pairs={{0,1},{1,0},{2,3},{3,2},{4,5},{5,4},{6,7},{7,6},{8,9},{9,8},{10,11... | collective-permute-start | bytes 393224 | tf_op jit(solution)/shard_map/ppermute | solution.py:173
  345.3 7.2 %copy-start.1 = (bf16[1024,1024]{1,0:T(8,128)(2,1)S(1)}, bf16[1024,1024]{1,0:T(8,128)(2,1)}, u32[]{:S(2)}) copy-start(bf16[1024,1024]{1,0:T(8,128)(2,1)} %param.10) | copy-start | bytes 6291460
Sparse Core Ops, SparseCore 0:
  35.7 78.8 all-gather.8
  219.7 51.4 all-gather.6
  273.4 49.0 all-gather.4

commit v4 on v3

--- a/solution.py
+++ b/solution.py
@@ -174,11 +174,8 @@
     ]
     mine = jnp.concatenate([jnp.where(first, a[:half], a[half:]) for a in parts], axis=1)
     total = jnp.dot(mine, out_weight, preferred_element_type=jnp.float32)
-    pw = parts[0].shape[1]
-    for p, a in enumerate(got):
-        total = total + jnp.dot(
-            a, w_other[p * pw : (p + 1) * pw], preferred_element_type=jnp.float32
-        )
+    for a, w in zip(got, w_other):
+        total = total + jnp.dot(a, w, preferred_element_type=jnp.float32)
     return total.astype(jnp.bfloat16)
 
 
@@ -216,9 +213,15 @@
     lower_mask = jnp.tril(jnp.ones((BLK, BLK), dtype=jnp.bool_))
 
     inner_prefix, shard_prod = exclusive_blocks(block_mats)
-    w_other = lax.ppermute(out_weight, "hg", SWAP) if groups == 2 else None
-    earlier_prod, v_all, w_other = lax.optimization_barrier(
-        (exclusive_shards(shard_prod, "ctx"), v_all, w_other)
+    parts = 2 if heads % 2 == 0 else 1
+    pw = width // parts
+    w_other = [None] * parts
+    if groups == 2:
+        w_other = [
+            lax.ppermute(out_weight[p * pw : (p + 1) * pw], "hg", SWAP) for p in range(parts)
+        ]
+    earlier_prod, v_all, w_other[0] = lax.optimization_barrier(
+        (exclusive_shards(shard_prod, "ctx"), v_all, w_other[0])
     )
 
     def in_shard(matrix):
@@ -233,8 +236,8 @@
     kt_glob = jnp.einsum(
         "hie,hfe->hfi", in_shard(k_local), earlier_prod, precision=HP
     ).reshape(width, rows).astype(jnp.bfloat16)
-    parts = 2 if heads % 2 == 0 else 1
-    pw = width // parts
+    if parts > 1:
+        kt_glob, w_other[1:] = lax.optimization_barrier((kt_glob, w_other[1:]))
     kt_parts = [
         lax.all_gather(kt_glob[p * pw : (p + 1) * pw], "ctx", axis=0, tiled=False)
         for p in range(parts)

time: 364 us -> 367 us (level)
  local copies, waits for them, and re-layouts: 15.5 us -> 21.6 us
  waiting for transfers between devices: 199 us -> 195 us
    slice x0 -> x1, local copies, waits for them, and re-layouts: none -> 5.99 us  [local(): out_weight[p * pw:(p + 1) * pw]]
    ppermute x1 -> x2, waiting for transfers between devices: 42.4 us -> 38.5 us  [local(): lax.ppermute(out_weight[p * pw:(p + 1) * pw], 'hg', SWAP)]
  transfers between devices with their start and end apart: 12 -> 13, of which waited for: 9 -> 9; matrix products, arithmetic and copies ran while one was open for 23% -> 26% of each run, Pallas kernels for 4% -> 4%
where the time goes in v4:
time: 367 us; the launch traced here: 363 us
  waiting for transfers between devices  195 us (53%)
  matrix products  82.4 us (22%)
  Pallas kernels  31.6 us (9%)
  local copies, waits for them, and re-layouts  21.6 us (6%)
  between operations  14.2 us (4%)
  starting transfers between devices  11.4 us (3%)
  other arithmetic  7.37 us (2%)
    all_gather x2, waiting for transfers between devices, local(): lax.all_gather(kt_glob[p * pw:(p + 1) * pw], 'ctx', axis=0, tiled=False)  70.8 us
    ppermute x4, waiting for transfers between devices, exclusive_shards(): lax.ppermute(acc, axis, [(i, i + shift) for i in range(length - shift)])  64 us
    ppermute x2, waiting for transfers between devices, local(): lax.ppermute(out_weight[p * pw:(p + 1) * pw], 'hg', SWAP)  38.5 us
    dot_general x20, matrix products, mm(): return jnp.einsum('...ij,...jk->...ik', a, b, precision=HP)  32.9 us
    pallas_call x2, Pallas kernels, flash_attend(): pl.pallas_call(kernel, grid_spec=grid_spec, out_shape=jax.ShapeDtypeStruc...  31.6 us
    ppermute x1, waiting for transfers between devices, exchange_heads(): lax.ppermute(jnp.where(first, stacked[:, :, 1], stacked[:, :, 0]), 'hg',...  17.2 us
    dot_general x2, matrix products, in_shard(): moved = jnp.einsum('hnid,hned->hnie', inblock, inner_prefix, precision=HP)  14.4 us
    unnamed x19, local copies, waits for them, and re-layouts  7.94 us
  transfers between devices with their start and end apart: 13, of which 9 were waited for; matrix products, arithmetic and copies ran while one was open for 26% of the time, Pallas kernels for 4%

profile of v4, /device:TPU:27, one launch (start us, length us, event | category | flops | bytes accessed | tf_op | source)
XLA Modules:
  0.0 363.0 jit_solution(2549008546947269944)
XLA Ops:
  6.5 1.6 stack.12
  9.0 1.4 stack.13
  10.5 1.4 stack.14
  13.8 1.5 select_bitcast_fusion.1
  15.3 1.3 collective-permute-start
  16.6 17.2 %collective-permute-done = bf16[128,3,1024]{2,0,1:T(8,128)(2,1)S(1)} collective-permute-done((bf16[128,3,1024]{2,0,1:T(8,128)(2,1)S(1)}, bf16[128,3,1024]{2,0,1:T(8,128)(2,1)S(1)}, u32[]{:S(2)}, u32[]{:S(2)}) %collective-permute-start) | collective-permute-done | bytes 786464 | tf_op jit(solution)/shard_map/ppermute | solution.py:154
  35.7 6.0 %fusion.49 = (bf16[512,4096]{1,0:T(8,128)(2,1)}, bf16[512,4096]{1,0:T(8,128)(2,1)}) fusion(bf16[1024,4096]{1,0:T(8,128)(2,1)} %param.11), kind=kLoop, calls=%fused_computation.94 | loop fusion | bytes 16777216 | tf_op jit(solution)/shard_map/slice | solution.py:221
  41.7 1.2 collective-permute-start.6
  43.0 2.2 multiply_reduce_fusion
  45.5 1.8 fusion.15
  47.3 1.2 fusion.52
  48.5 1.2 fusion.53
  49.6 1.2 fusion.54
  50.8 1.2 fusion.55
  52.0 1.2 fusion.56
  53.2 1.2 fusion.28
  54.4 1.2 fusion.26
  56.8 1.4 fusion.22
  62.9 7.1 %convolution_subtract_fusion = f32[8,8,128,128]{3,2,1,0:T(8,128)S(1)} fusion(f32[8,8,32,128]{3,2,1,0:T(8,128)S(1)} %bitcast.123, f32[8,8,32,128]{3,2,1,0:T(8,128)S(1)} %fusion.59, f32[128,128]{1,0:T(8,128)S(1)} %fusion.43), kind=kOutput, calls=%fused_computation.21 | convolution fusion | flops 403701760 | bytes 6356992 | tf_op jit(solution)/shard_map/hnkd,hnke->hnde/dot_general | solution.py:212
  70.9 4.7 %fusion.2 = f32[8,8,128,128]{3,2,1,0:T(8,128)S(1)} fusion(f32[8,1,128,128]{3,2,1,0:T(8,128)S(1)} %broadcast_in_dim.41, f32[8,7,128,128]{3,2,1,0:T(8,128)S(1)} %slice.92, f32[8,7,128,128]{3,2,1,0:T(8,128)S(1)} %fusion.13), kind=kOutput, calls=%fused_computation.9 | convolution fusion | flops 1612709888 | bytes 12058624 | tf_op jit(solution)/shard_map/...ij,...jk->...ik/dot_general | solution.py:17
  76.0 4.7 %fusion.4 = f32[8,8,128,128]{3,2,1,0:T(8,128)S(1)} fusion(f32[8,8,128,128]{3,2,1,0:T(8,128)S(1)} %fusion.2, f32[8,6,128,128]{3,2,1,0:T(8,128)S(1)} %slice.95, f32[8,2,128,128]{3,2,1,0:T(8,128)S(1)} %broadcast_in_dim_broadcast_in_dim.7), kind=kOutput, calls=%fused_computation.11 | convolution fusion | flops 1611661312 | bytes 12582912 | tf_op jit(solution)/shard_map/...ij,...jk->...ik/dot_general | solution.py:17
  81.2 4.9 %fusion.8 = f32[8,8,128,128]{3,2,1,0:T(8,128)S(1)} fusion(f32[8,8,128,128]{3,2,1,0:T(8,128)S(1)} %fusion.4, f32[8,4,128,128]{3,2,1,0:T(8,128)S(1)} %slice.96, f32[8,4,128,128]{3,2,1,0:T(8,128)S(1)} %broadcast_in_dim_broadcast_in_dim.6), kind=kOutput, calls=%fused_computation.15 | convolution fusion | flops 1611661312 | bytes 12582912 | tf_op jit(solution)/shard_map/...ij,...jk->...ik/dot_general | solution.py:17
  86.1 1.9 copy-done.2
  88.7 1.3 collective-permute-start.1
  90.3 3.7 %collective-permute-done.1 = f32[8,128,128]{2,1,0:T(8,128)} collective-permute-done((f32[8,128,128]{2,1,0:T(8,128)S(1)}, f32[8,128,128]{2,1,0:T(8,128)}, u32[]{:S(2)}, u32[]{:S(2)}) %collective-permute-start.1) | collective-permute-done | bytes 524320 | tf_op jit(solution)/shard_map/ppermute | solution.py:50
  95.0 1.3 collective-permute-start.2
  97.5 8.3 %collective-permute-done.2 = f32[8,128,128]{2,1,0:T(8,128)} collective-permute-done((f32[8,128,128]{2,1,0:T(8,128)S(1)}, f32[8,128,128]{2,1,0:T(8,128)}, u32[]{:S(2)}, u32[]{:S(2)}) %collective-permute-start.2) | collective-permute-done | bytes 524320 | tf_op jit(solution)/shard_map/ppermute | solution.py:54
  105.8 1.7 convolution_select_fusion.6
  107.5 1.3 collective-permute-start.3
  109.8 19.1 %collective-permute-done.3 = f32[8,128,128]{2,1,0:T(8,128)S(1)} collective-permute-done((f32[8,128,128]{2,1,0:T(8,128)S(1)}, f32[8,128,128]{2,1,0:T(8,128)S(1)}, u32[]{:S(2)}, u32[]{:S(2)}) %collective-permute-start.3) | collective-permute-done | bytes 524320 | tf_op jit(solution)/shard_map/ppermute | solution.py:54
  129.6 1.3 collective-permute-start.4
  130.9 1.8 fusion.60
  133.8 19.5 %collective-permute-done.4 = f32[8,128,128]{2,1,0:T(8,128)S(1)} collective-permute-done((f32[8,128,128]{2,1,0:T(8,128)S(1)}, f32[8,128,128]{2,1,0:T(8,128)S(1)}, u32[]{:S(2)}, u32[]{:S(2)}) %collective-permute-start.4) | collective-permute-done | bytes 524320 | tf_op jit(solution)/shard_map/ppermute | solution.py:54
  154.0 1.5 collective-permute-start.5
  156.2 7.7 %fusion.16 = f32[8,8,32,128]{3,2,1,0:T(8,128)} fusion(f32[8,8,128,128]{3,2,1,0:T(8,128)S(1)} %copy-done.3, f32[8,8,32,128]{3,0,2,1:T(8,128)S(1)} %copy_subtract_fusion), kind=kOutput, calls=%fused_computation.39 | convolution fusion | flops 402653184 | bytes 6291456 | tf_op jit(solution)/shard_map/hnid,hned->hnie/dot_general | solution.py:233
  163.9 17.0 %collective-permute-done.5 = f32[8,128,128]{2,1,0:T(8,128)S(1)} collective-permute-done((f32[8,128,128]{2,1,0:T(8,128)S(1)}, f32[8,128,128]{2,1,0:T(8,128)S(1)}, u32[]{:S(2)}, u32[]{:S(2)}) %collective-permute-start.5) | collective-permute-done | bytes 524320 | tf_op jit(solution)/shard_map/ppermute | solution.py:54
  181.7 2.3 convolution_convert_fusion
  183.9 38.5 %collective-permute-done.7 = bf16[512,4096]{1,0:T(8,128)(2,1)} collective-permute-done((bf16[512,4096]{1,0:T(8,128)(2,1)}, bf16[512,4096]{1,0:T(8,128)(2,1)}, u32[]{:S(2)}, u32[]{:S(2)}) %collective-permute-start.7) | collective-permute-done | bytes 4194336 | tf_op jit(solution)/shard_map/ppermute | solution.py:221
  225.2 1.8 fusion.57
  228.8 6.7 %fusion.18 = f32[8,8,32,128]{3,2,1,0:T(8,128)S(1)} fusion(f32[8,8,128,128]{3,2,1,0:T(8,128)S(1)} %copy-done.4, f32[8,8,32,128]{3,0,2,1:T(8,128)S(1)} %copy_subtract_fusion.1), kind=kOutput, calls=%fused_computation.41 | convolution fusion | flops 402653184 | bytes 6291456 | tf_op jit(solution)/shard_map/hnid,hned->hnie/dot_general | solution.py:233
  238.3 36.5 %all-gather.11.cloned.1.call-done = bf16[8192,256]{1,0:T(8,128)(2,1)} async-done(((bf16[512,256]{1,0:T(8,128)(2,1)}), bf16[8192,256]{1,0:T(8,128)(2,1)}) %all-gather.11.cloned.1.call-update) | async-done | bytes 4194320 | tf_op jit(solution)/shard_map/all_gather | solution.py:242
  274.8 16.0 %shard_map.65 = bf16[256,512]{1,0:T(8,128)(2,1)} custom-call(s32[1]{0:T(128)} %bitcast.c_ref, bf16[256,512]{1,0:T(8,128)(2,1)} %copy.25.q_ref, bf16[16,512,256]{2,1,0:T(8,128)(2,1)} %bitcast.135, bf16[16,256,1024]{2,1,0:T(8,128)(2,1)} %bitcast.128), custom_call_target="tpu_custom_call" | custom-call | tf_op jit(solution)/shard_map/pallas_call | solution.py:138
  291.8 34.3 %all-gather.9.cloned.1.call-done = bf16[8192,256]{1,0:T(8,128)(2,1)} async-done(((bf16[512,256]{1,0:T(8,128)(2,1)}), bf16[8192,256]{1,0:T(8,128)(2,1)}) %all-gather.9.cloned.1.call-update) | async-done | bytes 4194320 | tf_op jit(solution)/shard_map/all_gather | solution.py:242
  326.0 15.6 %shard_map.64 = bf16[256,512]{1,0:T(8,128)(2,1)} custom-call(s32[1]{0:T(128)} %bitcast.c_ref, bf16[256,512]{1,0:T(8,128)(2,1)} %copy.24.q_ref, bf16[16,512,256]{2,1,0:T(8,128)(2,1)} %bitcast.134, bf16[16,256,1024]{2,1,0:T(8,128)(2,1)} %bitcast.129), custom_call_target="tpu_custom_call" | custom-call | tf_op jit(solution)/shard_map/pallas_call | solution.py:138
  342.7 1.3 collective-permute-start.8
  344.2 4.6 %fusion.39 = f32[128,4096]{1,0:T(8,128)S(1)} fusion(bf16[1024,4096]{1,0:T(8,128)(2,1)} %param.11, bf16[128,512]{1,0:T(8,128)(2,1)S(1)} %get-tuple-element.31, bf16[128,512]{1,0:T(8,128)(2,1)S(1)} %get-tuple-element.33), kind=kOutput, calls=%fused_computation.75 | convolution fusion | flops 1074266112 | bytes 10747904 | tf_op jit(solution)/shard_map/dot_general | solution.py:176
  348.9 3.2 convolution_add_fusion.1
  352.0 3.9 %fusion.1 = bf16[128,4096]{1,0:T(8,128)(2,1)} fusion(f32[128,4096]{1,0:T(8,128)S(1)} %convolution_add_fusion.1, bf16[128,512]{1,0:T(8,128)(2,1)S(1)} %collective-permute-done.9, bf16[512,4096]{1,0:T(8,128)(2,1)} %collective-permute-done.7), kind=kOutput, calls=%fused_computation.7 | convolution fusion | flops 537919488 | bytes 7471104 | tf_op jit(solution)/shard_map/dot_general | solution.py:178
  (67 shorter events, 30.3 us)
Async XLA Ops:
  6.5 36.4 %copy-start = (bf16[1024,1024]{1,0:T(8,128)(2,1)S(1)}, bf16[1024,1024]{1,0:T(8,128)(2,1)}, u32[]{:S(2)}) copy-start(bf16[1024,1024]{1,0:T(8,128)(2,1)} %param.10) | copy-start | bytes 6291460
  6.5 175.1 %all-gather.7.cloned.1.call-start = ((), (), s32[]{:S(2)}) async-start(), calls=%async_computation | async-start | bytes 8912896 | tf_op jit(solution)/shard_map/all_gather | solution.py:194
  15.3 18.5 %collective-permute-start = (bf16[128,3,1024]{2,0,1:T(8,128)(2,1)S(1)}, bf16[128,3,1024]{2,0,1:T(8,128)(2,1)S(1)}, u32[]{:S(2)}, u32[]{:S(2)}) collective-permute-start(bf16[128,3,1024]{2,0,1:T(8,128)(2,1)S(1)} %get-tuple-element.25), channel_id=1, source_target_pairs={{0,1},{1,0},{2,3},{3,2},{4,5},{5,4},{6,7},{7,6},{8,9},{9,8},{10,11... | collective-permute-start | bytes 2359304 | tf_op jit(solution)/shard_map/ppermute | solution.py:154
  35.6 7.3 %copy-start.5 = (s32[256,8]{0,1:T(8,128)S(1)}, s32[256,8]{0,1:T(8,128)}, u32[]{:S(2)}) copy-start(s32[256,8]{0,1:T(8,128)} %param.9) | copy-start | bytes 24580
  35.6 239.2 %all-gather.11.cloned.1.call-start = ((), (), s32[]{:S(2)}) async-start(), calls=%async_computation.2 | async-start | bytes 4456448 | tf_op jit(solution)/shard_map/all_gather | solution.py:242
  41.7 140.0 %collective-permute-start.6 = (bf16[512,4096]{1,0:T(8,128)(2,1)}, bf16[512,4096]{1,0:T(8,128)(2,1)}, u32[]{:S(2)}, u32[]{:S(2)}) collective-permute-start(bf16[512,4096]{1,0:T(8,128)(2,1)} %get-tuple-element.20), channel_id=1, source_target_pairs={{0,1},{1,0},{2,3},{3,2},{4,5},{5,4},{6,7},{7,6},{8,9},{9,8},{10,11... | collective-permute-start | bytes 12582920 | tf_op jit(solution)/shard_map/ppermute | solution.py:221
  86.1 2.0 copy-start.2
  88.7 5.3 %collective-permute-start.1 = (f32[8,128,128]{2,1,0:T(8,128)S(1)}, f32[8,128,128]{2,1,0:T(8,128)}, u32[]{:S(2)}, u32[]{:S(2)}) collective-permute-start(f32[8,128,128]{2,1,0:T(8,128)S(1)} %fusion.31), channel_id=1, source_target_pairs={{0,2},{2,4},{4,6},{6,8},{8,10},{10,12},{12,14},{14,16},{16,18},{18... | collective-permute-start | bytes 1572872 | tf_op jit(solution)/shard_map/ppermute | solution.py:50
  90.0 132.4 %collective-permute-start.7 = (bf16[512,4096]{1,0:T(8,128)(2,1)}, bf16[512,4096]{1,0:T(8,128)(2,1)}, u32[]{:S(2)}, u32[]{:S(2)}) collective-permute-start(bf16[512,4096]{1,0:T(8,128)(2,1)} %get-tuple-element.19), channel_id=1, source_target_pairs={{0,1},{1,0},{2,3},{3,2},{4,5},{5,4},{6,7},{7,6},{8,9},{9,8},{10,11... | collective-permute-start | bytes 12582920 | tf_op jit(solution)/shard_map/ppermute | solution.py:221
  95.0 10.8 %collective-permute-start.2 = (f32[8,128,128]{2,1,0:T(8,128)S(1)}, f32[8,128,128]{2,1,0:T(8,128)}, u32[]{:S(2)}, u32[]{:S(2)}) collective-permute-start(f32[8,128,128]{2,1,0:T(8,128)S(1)} %broadcast_select_fusion), channel_id=1, source_target_pairs={{0,2},{2,4},{4,6},{6,8},{8,10},{10,12},{12,14},{14,16},{16,18},{18... | collective-permute-start | bytes 1572872 | tf_op jit(solution)/shard_map/ppermute | solution.py:54
  107.5 21.4 %collective-permute-start.3 = (f32[8,128,128]{2,1,0:T(8,128)S(1)}, f32[8,128,128]{2,1,0:T(8,128)S(1)}, u32[]{:S(2)}, u32[]{:S(2)}) collective-permute-start(f32[8,128,128]{2,1,0:T(8,128)S(1)} %convolution_select_fusion.6), channel_id=1, source_target_pairs={{0,4},{2,6},{4,8},{6,10},{8,12},{10,14},{12,16},{14,18},{16,20},{1... | collective-permute-start | bytes 1572872 | tf_op jit(solution)/shard_map/ppermute | solution.py:54
  129.6 23.8 %collective-permute-start.4 = (f32[8,128,128]{2,1,0:T(8,128)S(1)}, f32[8,128,128]{2,1,0:T(8,128)S(1)}, u32[]{:S(2)}, u32[]{:S(2)}) collective-permute-start(f32[8,128,128]{2,1,0:T(8,128)S(1)} %convolution_select_fusion.5), channel_id=1, source_target_pairs={{0,8},{2,10},{4,12},{6,14},{8,16},{10,18},{12,20},{14,22},{16,24},... | collective-permute-start | bytes 1572872 | tf_op jit(solution)/shard_map/ppermute | solution.py:54
  132.7 23.6 %copy-start.3 = (f32[8,8,128,128]{3,2,1,0:T(8,128)S(1)}, f32[8,8,128,128]{3,2,1,0:T(8,128)}, u32[]{:S(2)}) copy-start(f32[8,8,128,128]{3,2,1,0:T(8,128)} %copy-done.2) | copy-start | bytes 12582916
  154.0 26.9 %collective-permute-start.5 = (f32[8,128,128]{2,1,0:T(8,128)S(1)}, f32[8,128,128]{2,1,0:T(8,128)S(1)}, u32[]{:S(2)}, u32[]{:S(2)}) collective-permute-start(f32[8,128,128]{2,1,0:T(8,128)S(1)} %convolution_select_fusion.4), channel_id=1, source_target_pairs={{0,16},{2,18},{4,20},{6,22},{8,24},{10,26},{12,28},{14,30},{1,17},... | collective-permute-start | bytes 1572872 | tf_op jit(solution)/shard_map/ppermute | solution.py:54
  223.3 102.7 %all-gather.9.cloned.1.call-start = ((), (), s32[]{:S(2)}) async-start(), calls=%async_computation.1 | async-start | bytes 4456448 | tf_op jit(solution)/shard_map/all_gather | solution.py:242
  225.1 3.7 %copy-start.4 = (f32[8,8,128,128]{3,2,1,0:T(8,128)S(1)}, f32[8,8,128,128]{3,2,1,0:T(8,128)}, u32[]{:S(2)}) copy-start(f32[8,8,128,128]{3,2,1,0:T(8,128)} %copy-done.2) | copy-start | bytes 12582916
  342.7 6.2 %collective-permute-start.8 = (bf16[128,512]{1,0:T(8,128)(2,1)S(1)}, bf16[128,512]{1,0:T(8,128)(2,1)S(1)}, u32[]{:S(2)}, u32[]{:S(2)}) collective-permute-start(bf16[128,512]{1,0:T(8,128)(2,1)S(1)} %get-tuple-element.32), channel_id=1, source_target_pairs={{0,1},{1,0},{2,3},{3,2},{4,5},{5,4},{6,7},{7,6},{8,9},{9,8},{10,11... | collective-permute-start | bytes 393224 | tf_op jit(solution)/shard_map/ppermute | solution.py:173
  343.9 8.1 %collective-permute-start.9 = (bf16[128,512]{1,0:T(8,128)(2,1)S(1)}, bf16[128,512]{1,0:T(8,128)(2,1)S(1)}, u32[]{:S(2)}, u32[]{:S(2)}) collective-permute-start(bf16[128,512]{1,0:T(8,128)(2,1)S(1)} %get-tuple-element.30), channel_id=1, source_target_pairs={{0,1},{1,0},{2,3},{3,2},{4,5},{5,4},{6,7},{7,6},{8,9},{9,8},{10,11... | collective-permute-start | bytes 393224 | tf_op jit(solution)/shard_map/ppermute | solution.py:173
  348.8 7.1 %copy-start.1 = (bf16[1024,1024]{1,0:T(8,128)(2,1)S(1)}, bf16[1024,1024]{1,0:T(8,128)(2,1)}, u32[]{:S(2)}) copy-start(bf16[1024,1024]{1,0:T(8,128)(2,1)} %param.10) | copy-start | bytes 6291460
Sparse Core Ops, SparseCore 0:
  35.7 77.7 all-gather.6
  223.4 51.3 all-gather.10
  277.0 49.0 all-gather.8
